TPU v7x, 128 devices: a whole 4x4x4 slice. The times are simulated.
128 devices in a mesh: row: 8 (over y, core), col: 16 (over z, x).
Axes of the slice: x: 4, y: 4, z: 4, core: 2. Of those that a mesh axis runs over, the one named last changes fastest.
Arguments:
- mock_maps: bfloat16 [1024, 163840], P('col', 'row'), may hold values from -6 to 6
- window_blocks: int32 [4], replicated, may hold values from 0 to 127, as said below
- kept_tiles: int32 [128, 4], P(('row', 'col')), may hold values from 0 to 1, as said below
- taper_index: int32 [128, 4], P(('row', 'col')), may hold values from 0 to 3, as said below
- taper_table: float32 [4], replicated, may hold values from 0.25 to 2
Outputs:
- covariance: bfloat16 [163840, 5120], P(('row', 'col'))
Inputs may be any that keep to these rules, and one draw needn't show every extreme that they name: `window_blocks`: the entries are distinct feature blocks; the first and the last feature block are always among them. `kept_tiles`: A tile whose row block is its own window column block is always kept. `taper_index`: A tile whose row block is its own window column block takes entry 0.
All inputs are finite; a program needn't handle non-finite values.
Results may differ from a plain program's by a relative error of at most 0.001.
Values may be sent and summed in bfloat16 or wider, within the bound.
No kernel may reach another device: no remote copies, remote signals or barrier semaphores. Data moves between devices by JAX's collectives and lax.ppermute only.
A program may use at most 128 MiB of HBM per device.

v0:
```python
import jax
import jax.numpy as jnp
from jax import lax
from jax.sharding import PartitionSpec as P

WINDOW = 4


def spread(array, axis, root):
    mine = lax.axis_index(axis) == root
    return lax.psum(jnp.where(mine, array, jnp.zeros_like(array)), axis)


def per_device(mock_maps, window_blocks, kept_tiles, taper_index, taper_table):
    own_block = lax.all_to_all(mock_maps, "col", split_axis=1, concat_axis=0, tiled=True)
    mock_count = own_block.shape[0]
    block_width = own_block.shape[1]
    own_mean = jnp.sum(own_block, axis=0, dtype=jnp.float32) / mock_count
    product_list = []
    mean_list = []
    for slot in range(WINDOW):
        block_id = window_blocks[slot]
        column_panel = spread(own_block, ("row", "col"), block_id)
        mean_list.append(jnp.sum(column_panel, axis=0, dtype=jnp.float32) / mock_count)
        product_list.append(
            lax.dot_general(
                own_block,
                column_panel,
                (((0,), (0,)), ((), ())),
                preferred_element_type=jnp.float32,
            )
        )
    products = jnp.concatenate(product_list, axis=1)
    panel_mean = jnp.concatenate(mean_list, axis=0)
    classes = jnp.arange(taper_table.shape[0], dtype=jnp.int32)
    weights = jnp.sum(
        jnp.where(
            classes[None, :] == taper_index[0][:, None], taper_table[None, :], jnp.float32(0.0)
        ),
        axis=1,
    )
    weight_cols = jnp.repeat(weights, block_width)
    keep_cols = jnp.repeat(kept_tiles[0], block_width)
    centred = products - mock_count * own_mean[:, None] * panel_mean[None, :]
    tile_value = weight_cols[None, :] * centred / (mock_count - 1)
    tile_value = jnp.where(keep_cols[None, :] > 0, tile_value, jnp.float32(0.0))
    return tile_value.astype(jnp.bfloat16)


def solution(mesh):
    in_specs = (P("col", "row"), P(), P(("row", "col"), None), P(("row", "col"), None), P())
    out_specs = P(("row", "col"), None)
    return jax.shard_map(
        per_device, mesh=mesh, in_specs=in_specs, out_specs=out_specs, check_vma=False
    )
```

profile of v0, /device:TPU:1, one launch (start us, length us, event | category | flops | bytes accessed | tf_op | source)
XLA Modules:
  0.0 291.6 jit_solution(22568428264643381)
XLA Ops:
  6.5 3.5 %copy.16 = bf16[8,16,8,1280]{3,2,0,1:T(8,128)(2,1)} copy(bf16[8,16,8,1280]{3,2,1,0:T(8,128)(2,1)} %bitcast.40) | data formatting | bytes 5242880 | tf_op jit(solution)/shard_map/all_to_all | solution.py:15
  10.0 0.0 copy-start.4
  10.0 8.5 %all-to-all-start = ((bf16[64,16,1280]{2,0,1:T(8,128)(2,1)}), bf16[64,16,1280]{2,0,1:T(8,128)(2,1)S(1)}, u32[]{:S(2)}, u32[]{:S(2)}) async-start(bf16[64,16,1280]{2,0,1:T(8,128)(2,1)} %bitcast.39), calls=%async_computation | async-start | bytes 5242880 | tf_op jit(solution)/shard_map/all_to_all | solution.py:15
  18.6 0.0 all-reduce.3.cloned.1.call-start
  18.6 0.0 copy-done.4
  18.7 0.7 fusion.4
  21.8 35.8 %all-to-all-done = bf16[64,16,1280]{2,0,1:T(8,128)(2,1)S(1)} async-done(((bf16[64,16,1280]{2,0,1:T(8,128)(2,1)}), bf16[64,16,1280]{2,0,1:T(8,128)(2,1)S(1)}, u32[]{:S(2)}, u32[]{:S(2)}) %all-to-all-start) | async-done | bytes 2621472 | tf_op jit(solution)/shard_map/all_to_all | solution.py:15
  57.7 4.3 %broadcast_select_fusion.3 = (bf16[1024,1280]{1,0:T(8,128)(2,1)}, bf16[1024,1280]{1,0:T(8,128)(2,1)}, bf16[1024,1280]{1,0:T(8,128)(2,1)}, bf16[1024,1280]{1,0:T(8,128)(2,1)}) fusion(pred[]{:T(512)S(6)} %eq.31, bf16[64,16,1280]{2,0,1:T(8,128)(2,1)S(1)} %all-to-all-done, pred[]{:T(512)S(6)} %eq.32, pred[]{:T(512)S(6)} %eq.33, pred[]{:T(512)S(6)} %eq.34), kind=kLoop, calls=%fused_computation.18 | loop fusion | flops 5242880 | bytes 13107204 | tf_op jit(solution)/shard_map/jit(_where)/select_n | solution.py:11
  62.0 0.0 all-reduce.3.cloned.1.call-update
  62.0 0.6 copy-done.5
  62.6 0.1 broadcast_in_dim.34
  62.7 0.0 copy-done.6
  62.7 0.0 copy-done.7
  62.8 0.2 select_reduce_fusion
  62.9 0.1 broadcast_in_dim.38
  63.0 0.4 convert_reduce_fusion.4
  63.5 164.1 %all-reduce.3.cloned.1.call-done = (bf16[1024,1280]{1,0:T(8,128)(2,1)}, bf16[1024,1280]{1,0:T(8,128)(2,1)}, bf16[1024,1280]{1,0:T(8,128)(2,1)}, bf16[1024,1280]{1,0:T(8,128)(2,1)}) async-done(((bf16[1024,1280]{1,0:T(8,128)(2,1)}, bf16[1024,1280]{1,0:T(8,128)(2,1)}, bf16[1024,1280]{1,0:T(8,128)(2,1)}, bf16[1024,1280]{1,0:T(8,128)(2,1)}), (bf16[1024,1280]{1,0:T(8,128)(2,1)}, bf16[1024,1280]{1,0:T(8,128)(2,1)}, ...) | async-done | bytes 10485776 | tf_op jit(solution)/shard_map/psum | solution.py:11
  227.5 3.5 %convert_reduce_fusion.2 = (f32[1280]{0:T(1024)S(1)}, f32[1280]{0:T(1024)S(1)}) fusion(bf16[1024,1280]{1,0:T(8,128)(2,1)} %get-tuple-element.7, bf16[1024,1280]{1,0:T(8,128)(2,1)} %get-tuple-element.8), kind=kLoop, calls=%fused_computation.11 | loop fusion | flops 5240320 | bytes 5253120 | tf_op jit(solution)/shard_map/reduce_sum | solution.py:24
  231.0 0.0 copy-done.3
  231.0 0.0 copy-start.2
  231.0 3.7 %convolution_bitcast_fusion.3 = f32[1280,1280]{0,1:T(8,128)S(1)} fusion(bf16[1024,1280]{1,0:T(8,128)(2,1)S(1)} %copy-done.3, bf16[1024,1280]{1,0:T(8,128)(2,1)S(1)} %bitcast.35), kind=kOutput, calls=%fused_computation.8 | convolution fusion | flops 3355443200 | bytes 11796480 | tf_op jit(solution)/shard_map/dot_general | solution.py:26
  234.7 0.0 copy-done.2
  234.7 0.0 copy-start.1
  234.7 3.7 %convolution_bitcast_fusion.2 = f32[1280,1280]{0,1:T(8,128)S(1)} fusion(bf16[1024,1280]{1,0:T(8,128)(2,1)S(1)} %copy-done.2, bf16[1024,1280]{1,0:T(8,128)(2,1)S(1)} %bitcast.36), kind=kOutput, calls=%fused_computation.7 | convolution fusion | flops 3355443200 | bytes 11796480 | tf_op jit(solution)/shard_map/dot_general | solution.py:26
  238.4 0.0 copy-done.1
  238.4 0.0 copy-start
  238.4 5.7 %convolution_bitcast_fusion.1 = f32[1280,1280]{0,1:T(8,128)} fusion(bf16[1024,1280]{1,0:T(8,128)(2,1)S(1)} %copy-done.1, bf16[1024,1280]{1,0:T(8,128)(2,1)S(1)} %bitcast.37), kind=kOutput, calls=%fused_computation.6 | convolution fusion | flops 3355443200 | bytes 11796480 | tf_op jit(solution)/shard_map/dot_general | solution.py:26
  244.2 0.0 copy-done
  244.2 0.8 convert_reduce_fusion
  245.0 5.6 %convolution_bitcast_fusion = f32[1280,1280]{0,1:T(8,128)} fusion(bf16[1024,1280]{1,0:T(8,128)(2,1)S(1)} %copy-done, bf16[1024,1280]{1,0:T(8,128)(2,1)S(1)} %bitcast.38), kind=kOutput, calls=%fused_computation.5 | convolution fusion | flops 3355443200 | bytes 11796480 | tf_op jit(solution)/shard_map/dot_general | solution.py:26
  250.6 16.5 %fusion.3 = bf16[1280,5120]{0,1:T(8,128)(2,1)} fusion(f32[1280,1280]{0,1:T(8,128)} %convolution_bitcast_fusion, f32[1280,1280]{0,1:T(8,128)} %convolution_bitcast_fusion.1, f32[1280,1280]{0,1:T(8,128)S(1)} %convolution_bitcast_fusion.2, f32[1280,1280]{0,1:T(8,128)S(1)} %convolution_bitcast_fusion.3, f32[5120]{0:T(1024)S(1)} %pad_maximum_fusion, ...), kind=kLoop, calls=%fused_computation.4 | loop fusion | flops 58982400 | bytes 39372800 | tf_op jit(solution)/shard_map/convert_element_type | solution.py:47
  267.1 17.6 %copy.13 = bf16[1280,5120]{1,0:T(8,128)(2,1)} copy(bf16[1280,5120]{0,1:T(8,128)(2,1)} %fusion.3) | data formatting | bytes 26214400 | tf_op jit(solution)/shard_map/convert_element_type | solution.py:47
  (12 shorter events, 0.1 us)
Async XLA Ops:
  10.0 8.6 %copy-start.4 = (s32[4]{0:T(128)S(1)}, s32[4]{0:T(128)}, u32[]{:S(2)}) copy-start(s32[4]{0:T(128)} %param.6) | copy-start | bytes 52
  10.0 47.6 %all-to-all-start = ((bf16[64,16,1280]{2,0,1:T(8,128)(2,1)}), bf16[64,16,1280]{2,0,1:T(8,128)(2,1)S(1)}, u32[]{:S(2)}, u32[]{:S(2)}) async-start(bf16[64,16,1280]{2,0,1:T(8,128)(2,1)} %bitcast.39), calls=%async_computation | async-start | bytes 5242880 | tf_op jit(solution)/shard_map/all_to_all | solution.py:15
  18.6 208.9 %all-reduce.3.cloned.1.call-start = ((), (), s32[]{:S(2)}) async-start(), calls=%async_computation.1 | async-start | bytes 20971520 | tf_op jit(solution)/shard_map/psum | solution.py:11
  62.0 0.7 copy-start.5
  62.0 0.8 copy-start.6
  62.0 0.8 copy-start.7
  227.5 3.5 %copy-start.3 = (bf16[1024,1280]{1,0:T(8,128)(2,1)S(1)}, bf16[1024,1280]{1,0:T(8,128)(2,1)}, u32[]{:S(2)}) copy-start(bf16[1024,1280]{1,0:T(8,128)(2,1)} %get-tuple-element.8) | copy-start | bytes 7864324
  231.0 3.7 %copy-start.2 = (bf16[1024,1280]{1,0:T(8,128)(2,1)S(1)}, bf16[1024,1280]{1,0:T(8,128)(2,1)}, u32[]{:S(2)}) copy-start(bf16[1024,1280]{1,0:T(8,128)(2,1)} %get-tuple-element.7) | copy-start | bytes 7864324
  234.7 3.7 %copy-start.1 = (bf16[1024,1280]{1,0:T(8,128)(2,1)S(1)}, bf16[1024,1280]{1,0:T(8,128)(2,1)}, u32[]{:S(2)}) copy-start(bf16[1024,1280]{1,0:T(8,128)(2,1)} %get-tuple-element.6) | copy-start | bytes 7864324
  238.4 5.8 %copy-start = (bf16[1024,1280]{1,0:T(8,128)(2,1)S(1)}, bf16[1024,1280]{1,0:T(8,128)(2,1)}, u32[]{:S(2)}) copy-start(bf16[1024,1280]{1,0:T(8,128)(2,1)} %get-tuple-element.5) | copy-start | bytes 7864324
Sparse Core Ops, SparseCore 0:
  62.1 165.3 all-reduce.2
where the time goes:
time: 292 us
  waiting for transfers between devices  200 us (68%)
  other arithmetic  25.8 us (9%)
  local copies, waits for them, and re-layouts  22.6 us (8%)
  matrix products  18.6 us (6%)
  between operations  16 us (5%)
  starting transfers between devices  8.59 us (3%)
    psum x1, waiting for transfers between devices, spread(): return lax.psum(jnp.where(mine, array, jnp.zeros_like(array)), axis)  164 us
    all_to_all x1, waiting for transfers between devices, per_device(): lax.all_to_all(mock_maps, 'col', split_axis=1, concat_axis=0, tiled=True)  35.8 us
    dot_general x4, matrix products, per_device(): lax.dot_general(own_block, column_panel, (((0,), (0,)), ((), ())), prefer...  18.6 us
    convert_element_type x1, local copies, waits for them, and re-layouts, per_device(): return tile_value.astype(jnp.bfloat16)  17.6 us
    convert_element_type x1, other arithmetic, per_device(): return tile_value.astype(jnp.bfloat16)  16.5 us
    all_to_all x1, starting transfers between devices, per_device(): lax.all_to_all(mock_maps, 'col', split_axis=1, concat_axis=0, tiled=True)  8.55 us
  transfers between devices with their start and end apart: 2, of which 2 were waited for; matrix products, arithmetic and copies ran while one was open for 0% of the time, Pallas kernels for 0%

commit v1 on v0

v1 whole, which is shorter than its diff:
```python
import jax
import jax.numpy as jnp
from jax import lax
from jax.sharding import PartitionSpec as P

WINDOW = 4


def per_device(mock_maps, window_blocks, kept_tiles, taper_index, taper_table):
    block_width = mock_maps.shape[1] // lax.axis_size("col")
    local_blocks = mock_maps.shape[1] // block_width
    row = lax.axis_index("row")
    chunks = []
    for slot in range(WINDOW):
        local_id = window_blocks[slot] - row * local_blocks
        mine = (local_id >= 0) & (local_id < local_blocks)
        start = jnp.clip(local_id, 0, local_blocks - 1) * block_width
        piece = lax.dynamic_slice_in_dim(mock_maps, start, block_width, 1)
        chunks.append(jnp.where(mine, piece, jnp.zeros_like(piece)))
    local_panels = lax.psum(jnp.concatenate(chunks, axis=1), "row")
    panels = lax.all_gather(local_panels, "col", axis=0, tiled=True)

    own_block = lax.all_to_all(mock_maps, "col", split_axis=1, concat_axis=0, tiled=True)
    mock_count = own_block.shape[0]
    own_mean = jnp.sum(own_block, axis=0, dtype=jnp.float32) / mock_count
    panel_mean = jnp.sum(panels, axis=0, dtype=jnp.float32) / mock_count
    products = lax.dot_general(
        own_block, panels, (((0,), (0,)), ((), ())), preferred_element_type=jnp.float32
    )
    classes = jnp.arange(taper_table.shape[0], dtype=jnp.int32)
    weights = jnp.sum(
        jnp.where(
            classes[None, :] == taper_index[0][:, None], taper_table[None, :], jnp.float32(0.0)
        ),
        axis=1,
    )
    weight_cols = jnp.repeat(weights, block_width)
    keep_cols = jnp.repeat(kept_tiles[0], block_width)
    centred = products - mock_count * own_mean[:, None] * panel_mean[None, :]
    tile_value = weight_cols[None, :] * centred / (mock_count - 1)
    tile_value = jnp.where(keep_cols[None, :] > 0, tile_value, jnp.float32(0.0))
    return tile_value.astype(jnp.bfloat16)


def solution(mesh):
    in_specs = (P("col", "row"), P(), P(("row", "col"), None), P(("row", "col"), None), P())
    out_specs = P(("row", "col"), None)
    return jax.shard_map(
        per_device, mesh=mesh, in_specs=in_specs, out_specs=out_specs, check_vma=False
    )
```

time: 292 us -> 237 us (0.81)
  waiting for transfers between devices: 200 us -> 160 us
  other arithmetic: 25.8 us -> 8.38 us
    psum x1, waiting for transfers between devices: 164 us -> 62.7 us  [per_device(): local_panels = lax.psum(jnp.concatenate(chunks, axis=1), 'row')]
    all_gather x0 -> x1, waiting for transfers between devices: none -> 57.5 us  [per_device(): panels = lax.all_gather(local_panels, 'col', axis=0, tiled=True)]
    convert_element_type x1 -> x0, other arithmetic: 16.5 us -> none  [per_device(): return tile_value.astype(jnp.bfloat16)]
    all_to_all x1, waiting for transfers between devices: 35.8 us -> 39.3 us  [per_device(): lax.all_to_all(mock_maps, 'col', split_axis=1, concat_axis=0, tiled=True)]
    select_n x1, other arithmetic: 4.33 us -> 1.27 us  [per_device(): chunks.append(jnp.where(mine, piece, jnp.zeros_like(piece)))]
    dot_general x4 -> x1, matrix products: 18.6 us -> 20.5 us  [per_device(): lax.dot_general(own_block, panels, (((0,), (0,)), ((), ())), preferred_el...]
  transfers between devices with their start and end apart: 2 -> 3, of which waited for: 2 -> 3; matrix products, arithmetic and copies ran while one was open for 0% -> 2% of each run, Pallas kernels for 0% -> 0%
where the time goes in v1:
time: 237 us; the launch traced here: 236 us
  waiting for transfers between devices  160 us (68%)
  local copies, waits for them, and re-layouts  25.1 us (11%)
  matrix products  20.5 us (9%)
  between operations  15.9 us (7%)
  other arithmetic  8.38 us (4%)
  starting transfers between devices  6.71 us (3%)
    psum x1, waiting for transfers between devices, per_device(): local_panels = lax.psum(jnp.concatenate(chunks, axis=1), 'row')  62.7 us
    all_gather x1, waiting for transfers between devices, per_device(): panels = lax.all_gather(local_panels, 'col', axis=0, tiled=True)  57.5 us
    all_to_all x1, waiting for transfers between devices, per_device(): lax.all_to_all(mock_maps, 'col', split_axis=1, concat_axis=0, tiled=True)  39.3 us
    dot_general x1, matrix products, per_device(): lax.dot_general(own_block, panels, (((0,), (0,)), ((), ())), preferred_el...  20.5 us
    convert_element_type x1, local copies, waits for them, and re-layouts, per_device(): return tile_value.astype(jnp.bfloat16)  17.6 us
    all_to_all x1, starting transfers between devices, per_device(): lax.all_to_all(mock_maps, 'col', split_axis=1, concat_axis=0, tiled=True)  6.66 us
    reduce_sum x1, other arithmetic, per_device(): panel_mean = jnp.sum(panels, axis=0, dtype=jnp.float32) / mock_count  5.61 us
  transfers between devices with their start and end apart: 3, of which 3 were waited for; matrix products, arithmetic and copies ran while one was open for 2% of the time, Pallas kernels for 0%

profile of v1, /device:TPU:1, one launch (start us, length us, event | category | flops | bytes accessed | tf_op | source)
XLA Modules:
  0.0 236.2 jit_solution(14619275543654786151)
XLA Ops:
  6.5 0.0 copy-start.2
  6.5 0.0 copy-start.3
  6.5 0.0 copy-start.4
  6.5 0.0 all-reduce.2.cloned.1.call-start
  6.5 1.4 fusion.4
  10.4 1.3 dynamic-slice_select_fusion.3
  11.7 0.9 pad_maximum_fusion
  12.6 0.0 all-reduce.2.cloned.1.call-update
  12.6 0.0 all-gather.2.cloned.1.call-start
  12.7 62.7 %all-reduce.2.cloned.1.call-done = bf16[64,5120]{1,0:T(8,128)(2,1)} async-done(((bf16[64,5120]{1,0:T(8,128)(2,1)}), bf16[64,5120]{1,0:T(8,128)(2,1)}) %all-reduce.2.cloned.1.call-update) | async-done | bytes 655376 | tf_op jit(solution)/shard_map/psum | solution.py:20
  75.4 0.0 all-gather.2.cloned.1.call-update
  75.4 3.5 %copy.16 = bf16[8,16,8,1280]{3,2,0,1:T(8,128)(2,1)} copy(bf16[8,16,8,1280]{3,2,1,0:T(8,128)(2,1)} %bitcast.29) | data formatting | bytes 5242880 | tf_op jit(solution)/shard_map/all_to_all | solution.py:23
  78.9 6.7 %all-to-all-start = ((bf16[64,16,1280]{2,0,1:T(8,128)(2,1)}), bf16[64,16,1280]{2,0,1:T(8,128)(2,1)S(1)}, u32[]{:S(2)}, u32[]{:S(2)}) async-start(bf16[64,16,1280]{2,0,1:T(8,128)(2,1)} %bitcast.28), calls=%async_computation | async-start | bytes 5242880 | tf_op jit(solution)/shard_map/all_to_all | solution.py:23
  85.6 0.0 copy-done.2
  85.6 0.1 broadcast_in_dim.34
  85.7 0.0 copy-done.3
  85.7 0.0 copy-done.4
  85.7 0.2 select_reduce_fusion
  85.9 0.1 broadcast_in_dim.38
  86.0 39.3 %all-to-all-done = bf16[64,16,1280]{2,0,1:T(8,128)(2,1)S(1)} async-done(((bf16[64,16,1280]{2,0,1:T(8,128)(2,1)}), bf16[64,16,1280]{2,0,1:T(8,128)(2,1)S(1)}, u32[]{:S(2)}, u32[]{:S(2)}) %all-to-all-start) | async-done | bytes 2621472 | tf_op jit(solution)/shard_map/all_to_all | solution.py:23
  125.3 0.0 copy-start.1
  125.3 0.4 convert_reduce_fusion.1
  125.8 1.1 copy-done.1
  126.8 57.5 %all-gather.2.cloned.1.call-done = bf16[1024,5120]{1,0:T(8,128)(2,1)} async-done(((bf16[64,5120]{1,0:T(8,128)(2,1)}), bf16[1024,5120]{1,0:T(8,128)(2,1)}) %all-gather.2.cloned.1.call-update) | async-done | bytes 10485776 | tf_op jit(solution)/shard_map/all_gather | solution.py:21
  184.3 0.0 copy-start
  184.3 5.6 %convert_reduce_fusion = f32[5120]{0:T(1024)S(1)} fusion(bf16[1024,5120]{1,0:T(8,128)(2,1)} %all-gather.2.cloned.1.call-done), kind=kLoop, calls=%fused_computation.5 | loop fusion | flops 10480640 | bytes 10506240 | tf_op jit(solution)/shard_map/reduce_sum | solution.py:26
  189.9 1.3 copy-done
  191.3 20.5 %fusion.3 = bf16[1280,5120]{0,1:T(8,128)(2,1)} fusion(bf16[1024,5120]{1,0:T(8,128)(2,1)S(1)} %copy-done, bf16[1024,1280]{1,0:T(8,128)(2,1)} %bitcast.27, f32[5120]{0:T(1024)S(1)} %broadcast_multiply_fusion, f32[1280]{0:T(1024)S(1)} %convert_reduce_fusion.1, f32[5120]{0:T(1024)S(1)} %mul.45, pred[5120]{0:T(1024)(128)(4,1)S(1)} %gt.21), kind=kOutput, calls=%fused_computation.4 | convolution fusion | flops 13461094400 | bytes 26265600 | tf_op jit(solution)/shard_map/dot_general | solution.py:27
  211.7 17.6 %copy.13 = bf16[1280,5120]{1,0:T(8,128)(2,1)} copy(bf16[1280,5120]{0,1:T(8,128)(2,1)} %fusion.3) | data formatting | bytes 26214400 | tf_op jit(solution)/shard_map/convert_element_type | solution.py:42
  (4 shorter events, 0.0 us)
Async XLA Ops:
  6.5 79.1 %copy-start.2 = (s32[1,4]{1,0:T(1,128)S(1)}, s32[1,4]{1,0:T(1,128)}, u32[]{:S(2)}) copy-start(s32[1,4]{1,0:T(1,128)} %param.7) | copy-start | bytes 52
  6.5 79.2 %copy-start.3 = (f32[4]{0:T(128)S(1)}, f32[4]{0:T(128)}, u32[]{:S(2)}) copy-start(f32[4]{0:T(128)} %param.9) | copy-start | bytes 52
  6.5 79.2 %copy-start.4 = (s32[1,4]{1,0:T(1,128)S(1)}, s32[1,4]{1,0:T(1,128)}, u32[]{:S(2)}) copy-start(s32[1,4]{1,0:T(1,128)} %param.8) | copy-start | bytes 52
  6.5 68.9 %all-reduce.2.cloned.1.call-start = ((), (), s32[]{:S(2)}) async-start(), calls=%async_computation.1 | async-start | bytes 1310720 | tf_op jit(solution)/shard_map/psum | solution.py:20
  12.6 171.7 %all-gather.2.cloned.1.call-start = ((), (), s32[]{:S(2)}) async-start(), calls=%async_computation.2 | async-start | bytes 11141120 | tf_op jit(solution)/shard_map/all_gather | solution.py:21
  78.9 46.4 %all-to-all-start = ((bf16[64,16,1280]{2,0,1:T(8,128)(2,1)}), bf16[64,16,1280]{2,0,1:T(8,128)(2,1)S(1)}, u32[]{:S(2)}, u32[]{:S(2)}) async-start(bf16[64,16,1280]{2,0,1:T(8,128)(2,1)} %bitcast.28), calls=%async_computation | async-start | bytes 5242880 | tf_op jit(solution)/shard_map/all_to_all | solution.py:23
  125.3 1.5 copy-start.1
  184.3 7.0 %copy-start = (bf16[1024,5120]{1,0:T(8,128)(2,1)S(1)}, bf16[1024,5120]{1,0:T(8,128)(2,1)}, u32[]{:S(2)}) copy-start(bf16[1024,5120]{1,0:T(8,128)(2,1)} %all-gather.2.cloned.1.call-done) | copy-start | bytes 31457284
Sparse Core Ops, SparseCore 0:
  12.8 62.6 all-reduce.1
  77.5 106.7 all-gather.1

commit v2 on v1

--- a/solution.py
+++ b/solution.py
@@ -17,15 +17,17 @@
         start = jnp.clip(local_id, 0, local_blocks - 1) * block_width
         piece = lax.dynamic_slice_in_dim(mock_maps, start, block_width, 1)
         chunks.append(jnp.where(mine, piece, jnp.zeros_like(piece)))
-    local_panels = lax.psum(jnp.concatenate(chunks, axis=1), "row")
-    panels = lax.all_gather(local_panels, "col", axis=0, tiled=True)
+    local_panels = lax.psum_scatter(
+        jnp.concatenate(chunks, axis=1), "row", scatter_dimension=0, tiled=True
+    )
+    panels = lax.all_gather(local_panels, ("col", "row"), axis=0, tiled=True)
 
     own_block = lax.all_to_all(mock_maps, "col", split_axis=1, concat_axis=0, tiled=True)
     mock_count = own_block.shape[0]
     own_mean = jnp.sum(own_block, axis=0, dtype=jnp.float32) / mock_count
     panel_mean = jnp.sum(panels, axis=0, dtype=jnp.float32) / mock_count
     products = lax.dot_general(
-        own_block, panels, (((0,), (0,)), ((), ())), preferred_element_type=jnp.float32
+        own_block.T, panels, (((1,), (0,)), ((), ())), preferred_element_type=jnp.float32
     )
     classes = jnp.arange(taper_table.shape[0], dtype=jnp.int32)
     weights = jnp.sum(

time: 237 us -> 194 us (0.82)
  waiting for transfers between devices: 160 us -> 117 us
    psum x1 -> x0, waiting for transfers between devices: 62.7 us -> none  [per_device(): local_panels = lax.psum(jnp.concatenate(chunks, axis=1), 'row')]
    reduce_scatter x0 -> x1, waiting for transfers between devices: none -> 32.2 us  [per_device(): lax.psum_scatter(jnp.concatenate(chunks, axis=1), 'row', scatter_dimensio...]
    all_to_all x1, waiting for transfers between devices: 39.3 us -> 31.2 us  [per_device(): lax.all_to_all(mock_maps, 'col', split_axis=1, concat_axis=0, tiled=True)]
    all_gather x1, waiting for transfers between devices: 57.5 us -> 53.2 us  [per_device(): panels = lax.all_gather(local_panels, ('col', 'row'), axis=0, tiled=True)]
where the time goes in v2:
time: 194 us; the launch traced here: 193 us
  waiting for transfers between devices  117 us (60%)
  local copies, waits for them, and re-layouts  25.1 us (13%)
  matrix products  20.5 us (11%)
  between operations  15.9 us (8%)
  other arithmetic  8.38 us (4%)
  starting transfers between devices  6.81 us (4%)
    all_gather x1, waiting for transfers between devices, per_device(): panels = lax.all_gather(local_panels, ('col', 'row'), axis=0, tiled=True)  53.2 us
    reduce_scatter x1, waiting for transfers between devices, per_device(): lax.psum_scatter(jnp.concatenate(chunks, axis=1), 'row', scatter_dimensio...  32.2 us
    all_to_all x1, waiting for transfers between devices, per_device(): lax.all_to_all(mock_maps, 'col', split_axis=1, concat_axis=0, tiled=True)  31.2 us
    dot_general x1, matrix products, per_device(): lax.dot_general(own_block.T, panels, (((1,), (0,)), ((), ())), preferred_...  20.5 us
    convert_element_type x1, local copies, waits for them, and re-layouts, per_device(): return tile_value.astype(jnp.bfloat16)  17.6 us
    all_to_all x1, starting transfers between devices, per_device(): lax.all_to_all(mock_maps, 'col', split_axis=1, concat_axis=0, tiled=True)  6.77 us
    reduce_sum x1, other arithmetic, per_device(): panel_mean = jnp.sum(panels, axis=0, dtype=jnp.float32) / mock_count  5.61 us
  transfers between devices with their start and end apart: 3, of which 3 were waited for; matrix products, arithmetic and copies ran while one was open for 2% of the time, Pallas kernels for 0%

profile of v2, /device:TPU:1, one launch (start us, length us, event | category | flops | bytes accessed | tf_op | source)
XLA Modules:
  0.0 193.4 jit_solution(16813246661919364633)
XLA Ops:
  6.5 0.0 copy-start.2
  6.5 0.0 copy-start.3
  6.5 0.0 copy-start.4
  6.5 0.0 reduce-scatter.2.cloned.1.call-start
  6.5 1.4 fusion.4
  10.5 1.3 dynamic-slice_select_fusion.3
  11.7 0.9 pad_maximum_fusion
  12.6 0.0 reduce-scatter.2.cloned.1.call-update
  12.6 0.0 all-gather.2.cloned.1.call-start
  12.7 32.2 %reduce-scatter.2.cloned.1.call-done = bf16[8,5120]{1,0:T(8,128)(2,1)} async-done(((bf16[64,5120]{1,0:T(8,128)(2,1)}), bf16[8,5120]{1,0:T(8,128)(2,1)}) %reduce-scatter.2.cloned.1.call-update) | async-done | bytes 81936 | tf_op jit(solution)/shard_map/reduce_scatter | solution.py:20
  44.9 0.0 all-gather.2.cloned.1.call-update
  44.9 3.5 %copy.16 = bf16[8,16,8,1280]{3,2,0,1:T(8,128)(2,1)} copy(bf16[8,16,8,1280]{3,2,1,0:T(8,128)(2,1)} %bitcast.29) | data formatting | bytes 5242880 | tf_op jit(solution)/shard_map/all_to_all | solution.py:25
  48.4 6.8 %all-to-all-start = ((bf16[64,16,1280]{2,0,1:T(8,128)(2,1)}), bf16[64,16,1280]{2,0,1:T(8,128)(2,1)S(1)}, u32[]{:S(2)}, u32[]{:S(2)}) async-start(bf16[64,16,1280]{2,0,1:T(8,128)(2,1)} %bitcast.28), calls=%async_computation.1 | async-start | bytes 5242880 | tf_op jit(solution)/shard_map/all_to_all | solution.py:25
  55.2 0.0 copy-done.2
  55.2 0.1 broadcast_in_dim.34
  55.3 0.0 copy-done.3
  55.3 0.0 copy-done.4
  55.4 0.2 select_reduce_fusion
  55.5 0.1 broadcast_in_dim.38
  55.6 31.2 %all-to-all-done = bf16[64,16,1280]{2,0,1:T(8,128)(2,1)S(1)} async-done(((bf16[64,16,1280]{2,0,1:T(8,128)(2,1)}), bf16[64,16,1280]{2,0,1:T(8,128)(2,1)S(1)}, u32[]{:S(2)}, u32[]{:S(2)}) %all-to-all-start) | async-done | bytes 2621472 | tf_op jit(solution)/shard_map/all_to_all | solution.py:25
  86.9 0.0 copy-start.1
  86.9 0.4 convert_reduce_fusion.1
  87.3 1.1 copy-done.1
  88.4 53.2 %all-gather.2.cloned.1.call-done = bf16[1024,5120]{1,0:T(8,128)(2,1)} async-done(((bf16[8,5120]{1,0:T(8,128)(2,1)}), bf16[1024,5120]{1,0:T(8,128)(2,1)}) %all-gather.2.cloned.1.call-update) | async-done | bytes 10485776 | tf_op jit(solution)/shard_map/all_gather | solution.py:23
  141.6 0.0 copy-start
  141.6 5.6 %convert_reduce_fusion = f32[5120]{0:T(1024)S(1)} fusion(bf16[1024,5120]{1,0:T(8,128)(2,1)} %all-gather.2.cloned.1.call-done), kind=kLoop, calls=%fused_computation.5 | loop fusion | flops 10480640 | bytes 10506240 | tf_op jit(solution)/shard_map/reduce_sum | solution.py:28
  147.2 1.3 copy-done
  148.5 20.5 %fusion.3 = bf16[1280,5120]{0,1:T(8,128)(2,1)} fusion(bf16[1024,5120]{1,0:T(8,128)(2,1)S(1)} %copy-done, bf16[1024,1280]{1,0:T(8,128)(2,1)} %bitcast.27, f32[5120]{0:T(1024)S(1)} %broadcast_multiply_fusion, f32[1280]{0:T(1024)S(1)} %convert_reduce_fusion.1, f32[5120]{0:T(1024)S(1)} %mul.45, pred[5120]{0:T(1024)(128)(4,1)S(1)} %gt.21), kind=kOutput, calls=%fused_computation.4 | convolution fusion | flops 13461094400 | bytes 26265600 | tf_op jit(solution)/shard_map/dot_general | solution.py:29
  169.0 17.6 %copy.13 = bf16[1280,5120]{1,0:T(8,128)(2,1)} copy(bf16[1280,5120]{0,1:T(8,128)(2,1)} %fusion.3) | data formatting | bytes 26214400 | tf_op jit(solution)/shard_map/convert_element_type | solution.py:44
  (4 shorter events, 0.0 us)
Async XLA Ops:
  6.5 48.7 %copy-start.2 = (s32[1,4]{1,0:T(1,128)S(1)}, s32[1,4]{1,0:T(1,128)}, u32[]{:S(2)}) copy-start(s32[1,4]{1,0:T(1,128)} %param.7) | copy-start | bytes 52
  6.5 48.8 %copy-start.3 = (f32[4]{0:T(128)S(1)}, f32[4]{0:T(128)}, u32[]{:S(2)}) copy-start(f32[4]{0:T(128)} %param.9) | copy-start | bytes 52
  6.5 48.8 %copy-start.4 = (s32[1,4]{1,0:T(1,128)S(1)}, s32[1,4]{1,0:T(1,128)}, u32[]{:S(2)}) copy-start(s32[1,4]{1,0:T(1,128)} %param.8) | copy-start | bytes 52
  6.5 38.4 %reduce-scatter.2.cloned.1.call-start = ((), (), s32[]{:S(2)}) async-start(), calls=%async_computation.2 | async-start | bytes 737280 | tf_op jit(solution)/shard_map/reduce_scatter | solution.py:20
  12.6 128.9 %all-gather.2.cloned.1.call-start = ((), (), s32[]{:S(2)}) async-start(), calls=%async_computation.3 | async-start | bytes 10567680 | tf_op jit(solution)/shard_map/all_gather | solution.py:23
  48.4 38.4 %all-to-all-start = ((bf16[64,16,1280]{2,0,1:T(8,128)(2,1)}), bf16[64,16,1280]{2,0,1:T(8,128)(2,1)S(1)}, u32[]{:S(2)}, u32[]{:S(2)}) async-start(bf16[64,16,1280]{2,0,1:T(8,128)(2,1)} %bitcast.28), calls=%async_computation.1 | async-start | bytes 5242880 | tf_op jit(solution)/shard_map/all_to_all | solution.py:25
  86.9 1.5 copy-start.1
  141.6 7.0 %copy-start = (bf16[1024,5120]{1,0:T(8,128)(2,1)S(1)}, bf16[1024,5120]{1,0:T(8,128)(2,1)}, u32[]{:S(2)}) copy-start(bf16[1024,5120]{1,0:T(8,128)(2,1)} %all-gather.2.cloned.1.call-done) | copy-start | bytes 31457284
Sparse Core Ops, SparseCore 0:
  12.8 32.1 reduce-scatter.1
  48.1 93.4 all-gather.1

commit v3 on v2

--- a/solution.py
+++ b/solution.py
@@ -1,9 +1,47 @@
+import functools
+
 import jax
 import jax.numpy as jnp
 from jax import lax
+from jax.experimental import pallas as pl
+from jax.experimental.pallas import tpu as pltpu
 from jax.sharding import PartitionSpec as P
 
 WINDOW = 4
+TILE_N = 512
+
+
+def tile_kernel(mock_count, a_ref, b_ref, rows_ref, w_ref, keep_ref, o_ref):
+    b = b_ref[...]
+    prod = jnp.dot(a_ref[...], b, preferred_element_type=jnp.float32)
+    ones = jnp.ones((8, b.shape[0]), b.dtype)
+    col_sum = jnp.dot(ones, b, preferred_element_type=jnp.float32)[0:1, :]
+    centred = prod - rows_ref[...] * (col_sum / mock_count)
+    val = w_ref[...] * centred / (mock_count - 1)
+    o_ref[...] = jnp.where(keep_ref[...] > 0, val, jnp.float32(0.0)).astype(o_ref.dtype)
+
+
+def covariance_tiles(own_t, panels, row_sums, weight_cols, keep_cols):
+    fb, k = own_t.shape
+    n = panels.shape[1]
+    return pl.pallas_call(
+        functools.partial(tile_kernel, k),
+        grid=(n // TILE_N,),
+        in_specs=[
+            pl.BlockSpec((fb, k), lambda j: (0, 0)),
+            pl.BlockSpec((k, TILE_N), lambda j: (0, j)),
+            pl.BlockSpec((fb, 1), lambda j: (0, 0)),
+            pl.BlockSpec((1, TILE_N), lambda j: (0, j)),
+            pl.BlockSpec((1, TILE_N), lambda j: (0, j)),
+        ],
+        out_specs=pl.BlockSpec((fb, TILE_N), lambda j: (0, j)),
+        out_shape=jax.ShapeDtypeStruct((fb, n), jnp.bfloat16),
+        compiler_params=pltpu.CompilerParams(vmem_limit_bytes=48 * 1024 * 1024),
+        cost_estimate=pl.CostEstimate(
+            flops=2 * fb * k * n, bytes_accessed=fb * k * 2 + k * n * 2 + fb * n * 2,
+            transcendentals=0,
+        ),
+    )(own_t, panels, row_sums, weight_cols, keep_cols)
 
 
 def per_device(mock_maps, window_blocks, kept_tiles, taper_index, taper_table):
@@ -24,11 +62,7 @@
 
     own_block = lax.all_to_all(mock_maps, "col", split_axis=1, concat_axis=0, tiled=True)
     mock_count = own_block.shape[0]
-    own_mean = jnp.sum(own_block, axis=0, dtype=jnp.float32) / mock_count
-    panel_mean = jnp.sum(panels, axis=0, dtype=jnp.float32) / mock_count
-    products = lax.dot_general(
-        own_block.T, panels, (((1,), (0,)), ((), ())), preferred_element_type=jnp.float32
-    )
+    row_sums = jnp.sum(own_block, axis=0, dtype=jnp.float32)[:, None]
     classes = jnp.arange(taper_table.shape[0], dtype=jnp.int32)
     weights = jnp.sum(
         jnp.where(
@@ -36,12 +70,9 @@
         ),
         axis=1,
     )
-    weight_cols = jnp.repeat(weights, block_width)
-    keep_cols = jnp.repeat(kept_tiles[0], block_width)
-    centred = products - mock_count * own_mean[:, None] * panel_mean[None, :]
-    tile_value = weight_cols[None, :] * centred / (mock_count - 1)
-    tile_value = jnp.where(keep_cols[None, :] > 0, tile_value, jnp.float32(0.0))
-    return tile_value.astype(jnp.bfloat16)
+    weight_cols = jnp.repeat(weights, block_width)[None, :]
+    keep_cols = jnp.repeat(kept_tiles[0], block_width)[None, :]
+    return covariance_tiles(own_block.T, panels, row_sums, weight_cols, keep_cols)
 
 
 def solution(mesh):

time: 194 us -> 177 us (0.912)
  Pallas kernels: 0 us -> 29.3 us
  matrix products: 20.5 us -> 0 us
  local copies, waits for them, and re-layouts: 25.1 us -> 7.49 us
  other arithmetic: 8.38 us -> 2.81 us
  waiting for transfers between devices: 117 us -> 114 us
    pallas_call x0 -> x1, Pallas kernels: none -> 29.3 us  [covariance_tiles(): pl.pallas_call(functools.partial(tile_kernel, k), grid=(n // TILE_N,), in...]
    dot_general x1 -> x0, matrix products: 20.5 us -> none  [per_device(): lax.dot_general(own_block.T, panels, (((1,), (0,)), ((), ())), preferred_...]
    convert_element_type x1 -> x0, local copies, waits for them, and re-layouts: 17.6 us -> none  [per_device(): return tile_value.astype(jnp.bfloat16)]
    reduce_sum x2 -> x1, other arithmetic: 6.03 us -> 0.47 us  [per_device(): row_sums = jnp.sum(own_block, axis=0, dtype=jnp.float32)[:, None]]
    all_gather x1, waiting for transfers between devices: 53.2 us -> 50.4 us  [per_device(): panels = lax.all_gather(local_panels, ('col', 'row'), axis=0, tiled=True)]
    all_to_all x1 -> x2, local copies, waits for them, and re-layouts: 3.5 us -> 4.75 us  [per_device(): lax.all_to_all(mock_maps, 'col', split_axis=1, concat_axis=0, tiled=True)]
  transfers between devices with their start and end apart: 3 -> 3, of which waited for: 3 -> 3; matrix products, arithmetic and copies ran while one was open for 2% -> 3% of each run, Pallas kernels for 0% -> 0%
where the time goes in v3:
time: 177 us; the launch traced here: 176 us
  waiting for transfers between devices  114 us (64%)
  Pallas kernels  29.3 us (17%)
  between operations  16.1 us (9%)
  local copies, waits for them, and re-layouts  7.49 us (4%)
  starting transfers between devices  6.94 us (4%)
  other arithmetic  2.81 us (2%)
    all_gather x1, waiting for transfers between devices, per_device(): panels = lax.all_gather(local_panels, ('col', 'row'), axis=0, tiled=True)  50.4 us
    reduce_scatter x1, waiting for transfers between devices, per_device(): lax.psum_scatter(jnp.concatenate(chunks, axis=1), 'row', scatter_dimensio...  32.2 us
    all_to_all x1, waiting for transfers between devices, per_device(): lax.all_to_all(mock_maps, 'col', split_axis=1, concat_axis=0, tiled=True)  31.2 us
    pallas_call x1, Pallas kernels, covariance_tiles(): pl.pallas_call(functools.partial(tile_kernel, k), grid=(n // TILE_N,), in...  29.3 us
    all_to_all x1, starting transfers between devices, per_device(): lax.all_to_all(mock_maps, 'col', split_axis=1, concat_axis=0, tiled=True)  6.9 us
    all_to_all x2, local copies, waits for them, and re-layouts, per_device(): lax.all_to_all(mock_maps, 'col', split_axis=1, concat_axis=0, tiled=True)  4.75 us
  transfers between devices with their start and end apart: 3, of which 3 were waited for; matrix products, arithmetic and copies ran while one was open for 3% of the time, Pallas kernels for 0%

profile of v3, /device:TPU:1, one launch (start us, length us, event | category | flops | bytes accessed | tf_op | source)
XLA Modules:
  0.0 176.4 jit_solution(4146539193557140603)
XLA Ops:
  6.5 0.0 copy-start
  6.5 0.0 copy-start.2
  6.5 0.0 reduce-scatter.2.cloned.1.call-start
  6.5 1.5 fusion
  10.7 1.3 dynamic-slice_select_fusion.3
  12.0 0.9 pad_maximum_fusion
  12.9 0.0 reduce-scatter.2.cloned.1.call-update
  12.9 0.0 all-gather.2.cloned.1.call-start
  12.9 32.2 %reduce-scatter.2.cloned.1.call-done = bf16[8,5120]{1,0:T(8,128)(2,1)} async-done(((bf16[64,5120]{1,0:T(8,128)(2,1)}), bf16[8,5120]{1,0:T(8,128)(2,1)}) %reduce-scatter.2.cloned.1.call-update) | async-done | bytes 81936 | tf_op jit(solution)/shard_map/reduce_scatter | solution.py:58
  45.1 0.0 all-gather.2.cloned.1.call-update
  45.2 0.0 copy-done.2
  45.2 1.8 copy.22
  46.9 0.0 copy-start.3
  46.9 0.0 copy-start.4
  46.9 6.9 %all-to-all-start = ((bf16[64,16,1280]{2,0,1:T(8,128)(2,1)}), bf16[64,16,1280]{2,0,1:T(8,128)(2,1)S(1)}, u32[]{:S(2)}, u32[]{:S(2)}) async-start(bf16[64,16,1280]{2,0,1:T(8,128)(2,1)} %bitcast.28), calls=%async_computation | async-start | bytes 5242880 | tf_op jit(solution)/shard_map/all_to_all | solution.py:63
  53.8 0.0 copy-done.3
  53.9 0.0 copy-done.4
  53.9 0.2 select_reduce_fusion
  54.0 0.1 broadcast_bitcast_fusion.1
  54.2 0.0 copy-done
  54.2 0.1 broadcast_bitcast_fusion
  54.3 31.2 %all-to-all-done = bf16[64,16,1280]{2,0,1:T(8,128)(2,1)S(1)} async-done(((bf16[64,16,1280]{2,0,1:T(8,128)(2,1)}), bf16[64,16,1280]{2,0,1:T(8,128)(2,1)S(1)}, u32[]{:S(2)}, u32[]{:S(2)}) %all-to-all-start) | async-done | bytes 2621472 | tf_op jit(solution)/shard_map/all_to_all | solution.py:63
  85.4 0.0 copy-start.1
  85.4 0.5 convert_reduce_fusion
  85.9 0.2 broadcast_in_dim.28.rows_ref
  86.1 0.8 copy-done.1
  86.9 3.0 %copy.16 = bf16[1024,1280]{0,1:T(8,128)(2,1)S(1)} copy(bf16[1024,1280]{1,0:T(8,128)(2,1)} %bitcast.27) | data formatting | bytes 5242880 | tf_op jit(solution)/shard_map/all_to_all | solution.py:63
  89.9 50.4 %all-gather.2.cloned.1.call-done.b_ref = bf16[1024,5120]{1,0:T(8,128)(2,1)} async-done(((bf16[8,5120]{1,0:T(8,128)(2,1)}), bf16[1024,5120]{1,0:T(8,128)(2,1)}) %all-gather.2.cloned.1.call-update) | async-done | bytes 10485776 | tf_op jit(solution)/shard_map/all_gather | solution.py:61
  140.3 29.3 %shard_map.55 = bf16[1280,5120]{1,0:T(8,128)(2,1)} custom-call(bf16[1280,1024]{1,0:T(8,128)(2,1)S(1)} %bitcast.24, bf16[1024,5120]{1,0:T(8,128)(2,1)} %all-gather.2.cloned.1.call-done.b_ref, f32[1280,1]{1,0:T(8,128)S(1)} %broadcast_in_dim.28.rows_ref, f32[1,5120]{1,0:T(1,128)S(1)} %bitcast.25, s32[1,5120]{1,0:T(1,128)S(1)} %bitcast.26), custom_call_target="tpu_custom_call" | custom-call | flops 13421772800 | bytes 26214400 | tf_op jit(solution)/shard_map/pallas_call | solution.py:27
  (2 shorter events, 0.0 us)
Async XLA Ops:
  6.5 47.6 %copy-start = (s32[1,4]{1,0:T(1,128)S(1)}, s32[1,4]{1,0:T(1,128)}, u32[]{:S(2)}) copy-start(s32[1,4]{1,0:T(1,128)} %param.7) | copy-start | bytes 52
  6.5 38.6 %copy-start.2 = (bf16[64,20480]{1,0:T(8,128)(2,1)S(1)}, bf16[64,20480]{1,0:T(8,128)(2,1)}, u32[]{:S(2)}) copy-start(bf16[64,20480]{1,0:T(8,128)(2,1)} %param.5) | copy-start | bytes 7864324
  6.5 38.6 %reduce-scatter.2.cloned.1.call-start = ((), (), s32[]{:S(2)}) async-start(), calls=%async_computation.2 | async-start | bytes 737280 | tf_op jit(solution)/shard_map/reduce_scatter | solution.py:58
  12.9 127.4 %all-gather.2.cloned.1.call-start = ((), (), s32[]{:S(2)}) async-start(), calls=%async_computation.3 | async-start | bytes 10567680 | tf_op jit(solution)/shard_map/all_gather | solution.py:61
  46.9 6.9 %copy-start.3 = (f32[4]{0:T(128)S(1)}, f32[4]{0:T(128)}, u32[]{:S(2)}) copy-start(f32[4]{0:T(128)} %param.9) | copy-start | bytes 52
  46.9 6.9 %copy-start.4 = (s32[1,4]{1,0:T(1,128)S(1)}, s32[1,4]{1,0:T(1,128)}, u32[]{:S(2)}) copy-start(s32[1,4]{1,0:T(1,128)} %param.8) | copy-start | bytes 52
  46.9 38.5 %all-to-all-start = ((bf16[64,16,1280]{2,0,1:T(8,128)(2,1)}), bf16[64,16,1280]{2,0,1:T(8,128)(2,1)S(1)}, u32[]{:S(2)}, u32[]{:S(2)}) async-start(bf16[64,16,1280]{2,0,1:T(8,128)(2,1)} %bitcast.28), calls=%async_computation | async-start | bytes 5242880 | tf_op jit(solution)/shard_map/all_to_all | solution.py:63
  85.4 1.5 copy-start.1
Sparse Core Ops, SparseCore 0:
  13.0 32.0 reduce-scatter.1
  48.3 91.9 all-gather.1

commit v4 on v3

v4 whole, which is shorter than its diff:
```python
import functools

import jax
import jax.numpy as jnp
from jax import lax
from jax.experimental import pallas as pl
from jax.experimental.pallas import tpu as pltpu
from jax.sharding import Mesh
from jax.sharding import PartitionSpec as P

WINDOW = 4
TILE_N = 512


def tile_kernel(mock_count, off_ref, a_ref, b_ref, rows_ref, w_ref, keep_ref, *rest):
    o_ref = rest[-1]
    b = b_ref[...]
    prod = jnp.dot(a_ref[...], b, preferred_element_type=jnp.float32)
    ones = jnp.ones((8, b.shape[0]), b.dtype)
    col_sum = jnp.dot(ones, b, preferred_element_type=jnp.float32)[0:1, :]
    centred = prod - rows_ref[...] * (col_sum / mock_count)
    val = w_ref[...] * centred / (mock_count - 1)
    o_ref[...] = jnp.where(keep_ref[...] > 0, val, jnp.float32(0.0)).astype(o_ref.dtype)


def half_tiles(offset, own_t, panels_half, row_sums, weight_cols, keep_cols, prev=None):
    fb, k = own_t.shape
    tiles = panels_half.shape[1] // TILE_N
    n = weight_cols.shape[1]
    in_specs = [
        pl.BlockSpec((fb, k), lambda j, off: (0, 0)),
        pl.BlockSpec((k, TILE_N), lambda j, off: (0, j)),
        pl.BlockSpec((fb, 1), lambda j, off: (0, 0)),
        pl.BlockSpec((1, TILE_N), lambda j, off: (0, off[0] * tiles + j)),
        pl.BlockSpec((1, TILE_N), lambda j, off: (0, off[0] * tiles + j)),
    ]
    args = [offset, own_t, panels_half, row_sums, weight_cols, keep_cols]
    aliases = {}
    if prev is not None:
        in_specs.append(pl.BlockSpec(memory_space=pl.ANY))
        args.append(prev)
        aliases = {len(args) - 1: 0}
    grid_spec = pltpu.PrefetchScalarGridSpec(
        num_scalar_prefetch=1,
        grid=(tiles,),
        in_specs=in_specs,
        out_specs=pl.BlockSpec((fb, TILE_N), lambda j, off: (0, off[0] * tiles + j)),
    )
    return pl.pallas_call(
        functools.partial(tile_kernel, k),
        grid_spec=grid_spec,
        out_shape=jax.ShapeDtypeStruct((fb, n), jnp.bfloat16),
        input_output_aliases=aliases,
        compiler_params=pltpu.CompilerParams(vmem_limit_bytes=48 * 1024 * 1024),
        cost_estimate=pl.CostEstimate(
            flops=2 * fb * k * tiles * TILE_N,
            bytes_accessed=fb * k * 2 + k * tiles * TILE_N * 2 + fb * tiles * TILE_N * 2,
            transcendentals=0,
        ),
    )(*args)


def per_device(mock_maps, window_blocks, kept_tiles, taper_index, taper_table):
    block_width = mock_maps.shape[1] // lax.axis_size("col")
    local_blocks = mock_maps.shape[1] // block_width
    ny = lax.axis_size("y")
    ncore = lax.axis_size("core")
    core = lax.axis_index("core")
    row = lax.axis_index("y") * ncore + core
    chunks = []
    for slot in range(WINDOW):
        local_id = window_blocks[slot] - row * local_blocks
        mine = (local_id >= 0) & (local_id < local_blocks)
        start = jnp.clip(local_id, 0, local_blocks - 1) * block_width
        piece = lax.dynamic_slice_in_dim(mock_maps, start, block_width, 1)
        chunks.append(jnp.where(mine, piece, jnp.zeros_like(piece)))
    local = jnp.concatenate(chunks, axis=1)
    m, n = local.shape
    local = local.reshape(ny, m // ny, ncore, n // ncore).transpose(0, 2, 1, 3)
    local = local.reshape(m * ncore, n // ncore)
    part = lax.psum_scatter(local, ("y", "core"), scatter_dimension=0, tiled=True)
    own_half = lax.all_gather(part, ("col", "y"), axis=0, tiled=True)
    other_half = lax.ppermute(own_half, "core", [(0, 1), (1, 0)])

    own_block = lax.all_to_all(mock_maps, "col", split_axis=1, concat_axis=0, tiled=True)
    row_sums = jnp.sum(own_block, axis=0, dtype=jnp.float32)[:, None]
    classes = jnp.arange(taper_table.shape[0], dtype=jnp.int32)
    weights = jnp.sum(
        jnp.where(
            classes[None, :] == taper_index[0][:, None], taper_table[None, :], jnp.float32(0.0)
        ),
        axis=1,
    )
    weight_cols = jnp.repeat(weights, block_width)[None, :]
    keep_cols = jnp.repeat(kept_tiles[0], block_width)[None, :]
    own_t = own_block.T
    first = half_tiles(
        core.astype(jnp.int32).reshape(1), own_t, own_half, row_sums, weight_cols, keep_cols
    )
    return half_tiles(
        (1 - core).astype(jnp.int32).reshape(1),
        own_t, other_half, row_sums, weight_cols, keep_cols, prev=first,
    )


def solution(mesh):
    rows, cols = mesh.devices.shape
    devices = mesh.devices.reshape(rows // 2, 2, cols)
    split_mesh = Mesh(devices, ("y", "core", "col"))
    feature_rows = ("y", "core", "col")
    in_specs = (P("col", ("y", "core")), P(), P(feature_rows, None), P(feature_rows, None), P())
    out_specs = P(feature_rows, None)
    return jax.shard_map(
        per_device, mesh=split_mesh, in_specs=in_specs, out_specs=out_specs, check_vma=False
    )
```

time: 177 us -> 213 us (1.20)
  waiting for transfers between devices: 114 us -> 146 us
  local copies, waits for them, and re-layouts: 7.49 us -> 10.8 us
  Pallas kernels: 29.3 us -> 31.7 us
    all_gather x1, waiting for transfers between devices: 50.4 us -> 73.2 us  [per_device(): own_half = lax.all_gather(part, ('col', 'y'), axis=0, tiled=True)]
    all_to_all x1, waiting for transfers between devices: 31.2 us -> 40.3 us  [per_device(): lax.all_to_all(mock_maps, 'col', split_axis=1, concat_axis=0, tiled=True)]
    reshape x0 -> x2, local copies, waits for them, and re-layouts: none -> 3.3 us  [per_device(): local = local.reshape(ny, m // ny, ncore, n // ncore).transpose(0, 2, 1, 3)]
    all_to_all x1, starting transfers between devices: 6.9 us -> 4.35 us  [per_device(): lax.all_to_all(mock_maps, 'col', split_axis=1, concat_axis=0, tiled=True)]
    pallas_call x1 -> x2, Pallas kernels: 29.3 us -> 31.7 us  [half_tiles(): pl.pallas_call(functools.partial(tile_kernel, k), grid_spec=grid_spec, ou...]
    ppermute x0 -> x1, starting transfers between devices: none -> 2.15 us  [per_device(): other_half = lax.ppermute(own_half, 'core', [(0, 1), (1, 0)])]
  transfers between devices with their start and end apart: 3 -> 4, of which waited for: 3 -> 3; matrix products, arithmetic and copies ran while one was open for 3% -> 3% of each run, Pallas kernels for 0% -> 7%
where the time goes in v4:
time: 213 us
  waiting for transfers between devices  146 us (69%)
  Pallas kernels  31.7 us (15%)
  between operations  16.1 us (8%)
  local copies, waits for them, and re-layouts  10.8 us (5%)
  starting transfers between devices  6.54 us (3%)
    all_gather x1, waiting for transfers between devices, per_device(): own_half = lax.all_gather(part, ('col', 'y'), axis=0, tiled=True)  73.2 us
    all_to_all x1, waiting for transfers between devices, per_device(): lax.all_to_all(mock_maps, 'col', split_axis=1, concat_axis=0, tiled=True)  40.3 us
    reduce_scatter x1, waiting for transfers between devices, per_device(): lax.psum_scatter(local, ('y', 'core'), scatter_dimension=0, tiled=True)  32.2 us
    pallas_call x2, Pallas kernels, half_tiles(): pl.pallas_call(functools.partial(tile_kernel, k), grid_spec=grid_spec, ou...  31.7 us
    all_to_all x2, local copies, waits for them, and re-layouts, per_device(): lax.all_to_all(mock_maps, 'col', split_axis=1, concat_axis=0, tiled=True)  4.75 us
    all_to_all x1, starting transfers between devices, per_device(): lax.all_to_all(mock_maps, 'col', split_axis=1, concat_axis=0, tiled=True)  4.35 us
  transfers between devices with their start and end apart: 4, of which 3 were waited for; matrix products, arithmetic and copies ran while one was open for 3% of the time, Pallas kernels for 7%

profile of v4, /device:TPU:1, one launch (start us, length us, event | category | flops | bytes accessed | tf_op | source)
XLA Modules:
  0.0 212.8 jit_solution(9052227824771799773)
XLA Ops:
  6.5 0.0 copy-start
  6.5 0.0 reduce-scatter.2.cloned.1.call-start
  6.5 1.5 fusion
  10.6 1.3 dynamic-slice_select_fusion.3
  11.8 0.0 copy-start.2
  11.9 1.3 reshape.18
  13.2 2.0 copy.25
  15.2 0.0 reduce-scatter.2.cloned.1.call-update
  15.2 0.0 all-gather.2.cloned.1.call-start
  15.3 32.2 %reduce-scatter.2.cloned.1.call-done = bf16[16,2560]{1,0:T(8,128)(2,1)} async-done(((bf16[128,2560]{1,0:T(8,128)(2,1)}), bf16[16,2560]{1,0:T(8,128)(2,1)}) %reduce-scatter.2.cloned.1.call-update) | async-done | bytes 81936 | tf_op jit(solution)/shard_map/reduce_scatter | solution.py:81
  47.5 0.0 all-gather.2.cloned.1.call-update
  47.5 73.2 %all-gather.2.cloned.1.call-done.b_ref = bf16[1024,2560]{1,0:T(8,128)(2,1)} async-done(((bf16[16,2560]{1,0:T(8,128)(2,1)}), bf16[1024,2560]{1,0:T(8,128)(2,1)}) %all-gather.2.cloned.1.call-update) | async-done | bytes 5242896 | tf_op jit(solution)/shard_map/all_gather | solution.py:82
  120.7 2.1 %collective-permute-start = (bf16[1024,2560]{1,0:T(8,128)(2,1)}, bf16[1024,2560]{1,0:T(8,128)(2,1)}, u32[]{:S(2)}, u32[]{:S(2)}) collective-permute-start(bf16[1024,2560]{1,0:T(8,128)(2,1)} %all-gather.2.cloned.1.call-done.b_ref), channel_id=1, source_target_pairs={{0,16},{16,0},{1,17},{17,1},{2,18},{18,2},{3,19},{19,3},{4,20},{20... | collective-permute-start | bytes 15728648 | tf_op jit(solution)/shard_map/ppermute | solution.py:83
  122.8 0.0 copy-done.2
  122.8 1.8 copy.32
  124.6 0.0 copy-start.3
  124.6 0.0 copy-start.4
  124.6 4.4 %all-to-all-start = ((bf16[64,16,1280]{2,0,1:T(8,128)(2,1)}), bf16[64,16,1280]{2,0,1:T(8,128)(2,1)S(1)}, u32[]{:S(2)}, u32[]{:S(2)}) async-start(bf16[64,16,1280]{2,0,1:T(8,128)(2,1)} %bitcast.36), calls=%async_computation | async-start | bytes 5242880 | tf_op jit(solution)/shard_map/all_to_all | solution.py:85
  128.9 0.0 copy-done.3
  129.0 0.0 copy-done.4
  129.0 0.2 select_reduce_fusion
  129.2 0.1 broadcast_bitcast_fusion.1
  129.3 0.0 copy-done
  129.3 0.1 broadcast_bitcast_fusion
  129.4 40.3 %all-to-all-done = bf16[64,16,1280]{2,0,1:T(8,128)(2,1)S(1)} async-done(((bf16[64,16,1280]{2,0,1:T(8,128)(2,1)}), bf16[64,16,1280]{2,0,1:T(8,128)(2,1)S(1)}, u32[]{:S(2)}, u32[]{:S(2)}) %all-to-all-start) | async-done | bytes 2621472 | tf_op jit(solution)/shard_map/all_to_all | solution.py:85
  169.7 0.4 convert_reduce_fusion
  170.1 0.2 broadcast_in_dim.28.rows_ref
  170.4 0.8 copy-done.1
  171.2 3.0 %copy.24 = bf16[1024,1280]{0,1:T(8,128)(2,1)S(1)} copy(bf16[1024,1280]{1,0:T(8,128)(2,1)} %bitcast.35) | data formatting | bytes 5242880 | tf_op jit(solution)/shard_map/all_to_all | solution.py:85
  174.2 15.9 %shard_map.55.rest_0_ = bf16[1280,5120]{1,0:T(8,128)(2,1)} custom-call(s32[1]{0:T(128)} %bitcast.12.off_ref, bf16[1280,1024]{1,0:T(8,128)(2,1)S(1)} %bitcast.29, bf16[1024,2560]{1,0:T(8,128)(2,1)} %all-gather.2.cloned.1.call-done.b_ref, f32[1280,1]{1,0:T(8,128)S(1)} %broadcast_in_dim.28.rows_ref, f32[1,5120]{1,0:T(1,128)S(1)} %bitcast.31, s32[1,5120]{1,0:T(1,128)S(1)} %bitcast.33), custom_call_target="tpu_custom_call" | custom-call | flops 6710886400 | bytes 14417920 | tf_op jit(solution)/shard_map/pallas_call | solution.py:49
  190.1 0.0 collective-permute-done.b_ref
  190.1 15.9 %shard_map.56 = bf16[1280,5120]{1,0:T(8,128)(2,1)} custom-call(s32[1]{0:T(128)} %bitcast.off_ref, bf16[1280,1024]{1,0:T(8,128)(2,1)S(1)} %bitcast.30, bf16[1024,2560]{1,0:T(8,128)(2,1)} %collective-permute-done.b_ref, f32[1280,1]{1,0:T(8,128)S(1)} %broadcast_in_dim.28.rows_ref, f32[1,5120]{1,0:T(1,128)S(1)} %bitcast.32, ...), custom_call_target="tpu_custom_call", output_to_operand_aliasing={{}: (6, {})} | custom-call | flops 6710886400 | bytes 14417920 | tf_op jit(solution)/shard_map/pallas_call | solution.py:49
  (4 shorter events, 0.1 us)
Async XLA Ops:
  6.5 122.7 %copy-start = (s32[1,4]{1,0:T(1,128)S(1)}, s32[1,4]{1,0:T(1,128)}, u32[]{:S(2)}) copy-start(s32[1,4]{1,0:T(1,128)} %param.7) | copy-start | bytes 52
  6.5 41.0 %reduce-scatter.2.cloned.1.call-start = ((), (), s32[]{:S(2)}) async-start(), calls=%async_computation.2 | async-start | bytes 737280 | tf_op jit(solution)/shard_map/reduce_scatter | solution.py:81
  11.8 111.0 %copy-start.2 = (bf16[64,20480]{1,0:T(8,128)(2,1)S(1)}, bf16[64,20480]{1,0:T(8,128)(2,1)}, u32[]{:S(2)}) copy-start(bf16[64,20480]{1,0:T(8,128)(2,1)} %param.5) | copy-start | bytes 7864324
  15.2 105.4 %all-gather.2.cloned.1.call-start = ((), (), s32[]{:S(2)}) async-start(), calls=%async_computation.3 | async-start | bytes 5324800 | tf_op jit(solution)/shard_map/all_gather | solution.py:82
  120.7 69.4 %collective-permute-start = (bf16[1024,2560]{1,0:T(8,128)(2,1)}, bf16[1024,2560]{1,0:T(8,128)(2,1)}, u32[]{:S(2)}, u32[]{:S(2)}) collective-permute-start(bf16[1024,2560]{1,0:T(8,128)(2,1)} %all-gather.2.cloned.1.call-done.b_ref), channel_id=1, source_target_pairs={{0,16},{16,0},{1,17},{17,1},{2,18},{18,2},{3,19},{19,3},{4,20},{20... | collective-permute-start | bytes 15728648 | tf_op jit(solution)/shard_map/ppermute | solution.py:83
  124.6 4.4 %copy-start.3 = (f32[4]{0:T(128)S(1)}, f32[4]{0:T(128)}, u32[]{:S(2)}) copy-start(f32[4]{0:T(128)} %param.9) | copy-start | bytes 52
  124.6 4.4 %copy-start.4 = (s32[1,4]{1,0:T(1,128)S(1)}, s32[1,4]{1,0:T(1,128)}, u32[]{:S(2)}) copy-start(s32[1,4]{1,0:T(1,128)} %param.8) | copy-start | bytes 52
  124.6 45.1 %all-to-all-start = ((bf16[64,16,1280]{2,0,1:T(8,128)(2,1)}), bf16[64,16,1280]{2,0,1:T(8,128)(2,1)S(1)}, u32[]{:S(2)}, u32[]{:S(2)}) async-start(bf16[64,16,1280]{2,0,1:T(8,128)(2,1)} %bitcast.36), calls=%async_computation | async-start | bytes 5242880 | tf_op jit(solution)/shard_map/all_to_all | solution.py:85
  169.7 1.5 copy-start.1
Sparse Core Ops, SparseCore 0:
  15.4 32.0 reduce-scatter.1
  50.4 70.2 all-gather.1

commit v5 on v4

--- a/solution.py
+++ b/solution.py
@@ -60,7 +60,7 @@
     )(*args)
 
 
-def per_device(mock_maps, window_blocks, kept_tiles, taper_index, taper_table):
+def device_body(mock_maps, window_blocks, kept_tiles, taper_index, taper_table):
     block_width = mock_maps.shape[1] // lax.axis_size("col")
     local_blocks = mock_maps.shape[1] // block_width
     ny = lax.axis_size("y")
@@ -78,7 +78,8 @@
     m, n = local.shape
     local = local.reshape(ny, m // ny, ncore, n // ncore).transpose(0, 2, 1, 3)
     local = local.reshape(m * ncore, n // ncore)
-    part = lax.psum_scatter(local, ("y", "core"), scatter_dimension=0, tiled=True)
+    sent = lax.all_to_all(local, ("y", "core"), split_axis=0, concat_axis=0, tiled=True)
+    part = jnp.sum(sent.reshape(ny * ncore, m // ny, n // ncore), axis=0, dtype=sent.dtype)
     own_half = lax.all_gather(part, ("col", "y"), axis=0, tiled=True)
     other_half = lax.ppermute(own_half, "core", [(0, 1), (1, 0)])
 
@@ -111,5 +112,5 @@
     in_specs = (P("col", ("y", "core")), P(), P(feature_rows, None), P(feature_rows, None), P())
     out_specs = P(feature_rows, None)
     return jax.shard_map(
-        per_device, mesh=split_mesh, in_specs=in_specs, out_specs=out_specs, check_vma=False
+        device_body, mesh=split_mesh, in_specs=in_specs, out_specs=out_specs, check_vma=False
     )

time: 213 us -> 194 us (0.911)
  waiting for transfers between devices: 146 us -> 110 us
  blocking collectives: 0 us -> 16.7 us
    reduce_scatter x1 -> x0, waiting for transfers between devices: 32.2 us -> none  [per_device(): lax.psum_scatter(local, ('y', 'core'), scatter_dimension=0, tiled=True)]
    all_to_all x0 -> x1, blocking collectives: none -> 16.7 us  [device_body(): lax.all_to_all(local, ('y', 'core'), split_axis=0, concat_axis=0, tiled=T...]
    all_gather x1, waiting for transfers between devices: 73.2 us -> 69.5 us  [device_body(): own_half = lax.all_gather(part, ('col', 'y'), axis=0, tiled=True)]
  transfers between devices with their start and end apart: 4 -> 3, of which waited for: 3 -> 2; matrix products, arithmetic and copies ran while one was open for 3% -> 3% of each run, Pallas kernels for 7% -> 8%
where the time goes in v5:
time: 194 us; the launch traced here: 193 us
  waiting for transfers between devices  110 us (57%)
  Pallas kernels  31.7 us (16%)
  blocking collectives  16.7 us (9%)
  between operations  16.1 us (8%)
  local copies, waits for them, and re-layouts  9.92 us (5%)
  starting transfers between devices  6.5 us (3%)
  other arithmetic  2.68 us (1%)
    all_gather x1, waiting for transfers between devices, device_body(): own_half = lax.all_gather(part, ('col', 'y'), axis=0, tiled=True)  69.5 us
    all_to_all x1, waiting for transfers between devices, device_body(): lax.all_to_all(mock_maps, 'col', split_axis=1, concat_axis=0, tiled=True)  40.3 us
    pallas_call x2, Pallas kernels, half_tiles(): pl.pallas_call(functools.partial(tile_kernel, k), grid_spec=grid_spec, ou...  31.7 us
    all_to_all x1, blocking collectives, device_body(): lax.all_to_all(local, ('y', 'core'), split_axis=0, concat_axis=0, tiled=T...  16.7 us
    all_to_all x2, local copies, waits for them, and re-layouts, device_body(): lax.all_to_all(mock_maps, 'col', split_axis=1, concat_axis=0, tiled=True)  4.75 us
    all_to_all x1, starting transfers between devices, device_body(): lax.all_to_all(mock_maps, 'col', split_axis=1, concat_axis=0, tiled=True)  4.35 us
  transfers between devices with their start and end apart: 3, of which 2 were waited for; matrix products, arithmetic and copies ran while one was open for 3% of the time, Pallas kernels for 8%

profile of v5, /device:TPU:1, one launch (start us, length us, event | category | flops | bytes accessed | tf_op | source)
XLA Modules:
  0.0 193.4 jit_solution(18095968300328145936)
XLA Ops:
  6.5 0.0 copy-start
  6.5 0.0 all-gather.2.cloned.1.call-start
  6.5 1.5 fusion
  10.6 1.3 dynamic-slice_select_fusion.3
  11.9 0.0 copy-start.2
  11.9 1.3 reshape.21
  13.2 1.2 copy.23
  14.4 16.7 %all_to_all.28 = bf16[8,16,2560]{2,1,0:T(8,128)(2,1)S(1)} all-to-all(bf16[8,16,2560]{2,1,0:T(8,128)(2,1)S(1)} %bitcast.38), channel_id=1, replica_groups=mesh['y'=4,'core'=2,'col'=16] {'y','core'}, dimensions={0} | all-to-all | bytes 1310720 | tf_op jit(solution)/shard_map/all_to_all | solution.py:81
  31.0 0.7 reduce_sum.27
  31.8 0.0 all-gather.2.cloned.1.call-update
  31.8 69.5 %all-gather.2.cloned.1.call-done.b_ref = bf16[1024,2560]{1,0:T(8,128)(2,1)} async-done(((bf16[16,2560]{1,0:T(8,128)(2,1)}), bf16[1024,2560]{1,0:T(8,128)(2,1)}) %all-gather.2.cloned.1.call-update) | async-done | bytes 5242896 | tf_op jit(solution)/shard_map/all_gather | solution.py:83
  101.3 2.1 %collective-permute-start = (bf16[1024,2560]{1,0:T(8,128)(2,1)}, bf16[1024,2560]{1,0:T(8,128)(2,1)}, u32[]{:S(2)}, u32[]{:S(2)}) collective-permute-start(bf16[1024,2560]{1,0:T(8,128)(2,1)} %all-gather.2.cloned.1.call-done.b_ref), channel_id=1, source_target_pairs={{0,16},{16,0},{1,17},{17,1},{2,18},{18,2},{3,19},{19,3},{4,20},{20... | collective-permute-start | bytes 15728648 | tf_op jit(solution)/shard_map/ppermute | solution.py:84
  103.5 0.0 copy-done.2
  103.5 1.8 copy.30
  105.2 0.0 copy-start.3
  105.2 0.0 copy-start.4
  105.2 4.4 %all-to-all-start = ((bf16[64,16,1280]{2,0,1:T(8,128)(2,1)}), bf16[64,16,1280]{2,0,1:T(8,128)(2,1)S(1)}, u32[]{:S(2)}, u32[]{:S(2)}) async-start(bf16[64,16,1280]{2,0,1:T(8,128)(2,1)} %bitcast.35), calls=%async_computation | async-start | bytes 5242880 | tf_op jit(solution)/shard_map/all_to_all | solution.py:86
  109.6 0.0 copy-done.3
  109.6 0.0 copy-done.4
  109.6 0.2 select_reduce_fusion
  109.8 0.1 broadcast_bitcast_fusion.1
  109.9 0.0 copy-done
  109.9 0.1 broadcast_bitcast_fusion
  110.0 40.3 %all-to-all-done = bf16[64,16,1280]{2,0,1:T(8,128)(2,1)S(1)} async-done(((bf16[64,16,1280]{2,0,1:T(8,128)(2,1)}), bf16[64,16,1280]{2,0,1:T(8,128)(2,1)S(1)}, u32[]{:S(2)}, u32[]{:S(2)}) %all-to-all-start) | async-done | bytes 2621472 | tf_op jit(solution)/shard_map/all_to_all | solution.py:86
  150.3 0.0 copy-start.1
  150.3 0.4 convert_reduce_fusion
  150.8 0.2 broadcast_in_dim.28.rows_ref
  151.0 0.8 copy-done.1
  151.8 3.0 %copy.22 = bf16[1024,1280]{0,1:T(8,128)(2,1)S(1)} copy(bf16[1024,1280]{1,0:T(8,128)(2,1)} %bitcast.34) | data formatting | bytes 5242880 | tf_op jit(solution)/shard_map/all_to_all | solution.py:86
  154.8 15.9 %shard_map.55.rest_0_ = bf16[1280,5120]{1,0:T(8,128)(2,1)} custom-call(s32[1]{0:T(128)} %bitcast.12.off_ref, bf16[1280,1024]{1,0:T(8,128)(2,1)S(1)} %bitcast.28, bf16[1024,2560]{1,0:T(8,128)(2,1)} %all-gather.2.cloned.1.call-done.b_ref, f32[1280,1]{1,0:T(8,128)S(1)} %broadcast_in_dim.28.rows_ref, f32[1,5120]{1,0:T(1,128)S(1)} %bitcast.30, s32[1,5120]{1,0:T(1,128)S(1)} %bitcast.32), custom_call_target="tpu_custom_call" | custom-call | flops 6710886400 | bytes 14417920 | tf_op jit(solution)/shard_map/pallas_call | solution.py:49
  170.7 0.0 collective-permute-done.b_ref
  170.7 15.9 %shard_map.56 = bf16[1280,5120]{1,0:T(8,128)(2,1)} custom-call(s32[1]{0:T(128)} %bitcast.off_ref, bf16[1280,1024]{1,0:T(8,128)(2,1)S(1)} %bitcast.29, bf16[1024,2560]{1,0:T(8,128)(2,1)} %collective-permute-done.b_ref, f32[1280,1]{1,0:T(8,128)S(1)} %broadcast_in_dim.28.rows_ref, f32[1,5120]{1,0:T(1,128)S(1)} %bitcast.31, ...), custom_call_target="tpu_custom_call", output_to_operand_aliasing={{}: (6, {})} | custom-call | flops 6710886400 | bytes 14417920 | tf_op jit(solution)/shard_map/pallas_call | solution.py:49
  (3 shorter events, 0.1 us)
Async XLA Ops:
  6.5 103.3 %copy-start = (s32[1,4]{1,0:T(1,128)S(1)}, s32[1,4]{1,0:T(1,128)}, u32[]{:S(2)}) copy-start(s32[1,4]{1,0:T(1,128)} %param.7) | copy-start | bytes 52
  6.5 94.8 %all-gather.2.cloned.1.call-start = ((), (), s32[]{:S(2)}) async-start(), calls=%async_computation.2 | async-start | bytes 5324800 | tf_op jit(solution)/shard_map/all_gather | solution.py:83
  11.9 91.5 %copy-start.2 = (bf16[64,20480]{1,0:T(8,128)(2,1)S(1)}, bf16[64,20480]{1,0:T(8,128)(2,1)}, u32[]{:S(2)}) copy-start(bf16[64,20480]{1,0:T(8,128)(2,1)} %param.5) | copy-start | bytes 7864324
  101.3 69.4 %collective-permute-start = (bf16[1024,2560]{1,0:T(8,128)(2,1)}, bf16[1024,2560]{1,0:T(8,128)(2,1)}, u32[]{:S(2)}, u32[]{:S(2)}) collective-permute-start(bf16[1024,2560]{1,0:T(8,128)(2,1)} %all-gather.2.cloned.1.call-done.b_ref), channel_id=1, source_target_pairs={{0,16},{16,0},{1,17},{17,1},{2,18},{18,2},{3,19},{19,3},{4,20},{20... | collective-permute-start | bytes 15728648 | tf_op jit(solution)/shard_map/ppermute | solution.py:84
  105.2 4.4 %copy-start.3 = (f32[4]{0:T(128)S(1)}, f32[4]{0:T(128)}, u32[]{:S(2)}) copy-start(f32[4]{0:T(128)} %param.9) | copy-start | bytes 52
  105.2 4.4 %copy-start.4 = (s32[1,4]{1,0:T(1,128)S(1)}, s32[1,4]{1,0:T(1,128)}, u32[]{:S(2)}) copy-start(s32[1,4]{1,0:T(1,128)} %param.8) | copy-start | bytes 52
  105.2 45.1 %all-to-all-start = ((bf16[64,16,1280]{2,0,1:T(8,128)(2,1)}), bf16[64,16,1280]{2,0,1:T(8,128)(2,1)S(1)}, u32[]{:S(2)}, u32[]{:S(2)}) async-start(bf16[64,16,1280]{2,0,1:T(8,128)(2,1)} %bitcast.35), calls=%async_computation | async-start | bytes 5242880 | tf_op jit(solution)/shard_map/all_to_all | solution.py:86
  150.3 1.5 copy-start.1
Sparse Core Ops, SparseCore 0:
  31.9 69.3 all-gather.1

commit v6 on v5

--- a/solution.py
+++ b/solution.py
@@ -9,7 +9,7 @@
 from jax.sharding import PartitionSpec as P
 
 WINDOW = 4
-TILE_N = 512
+TILE_N = 640
 
 
 def tile_kernel(mock_count, off_ref, a_ref, b_ref, rows_ref, w_ref, keep_ref, *rest):
@@ -19,7 +19,7 @@
     ones = jnp.ones((8, b.shape[0]), b.dtype)
     col_sum = jnp.dot(ones, b, preferred_element_type=jnp.float32)[0:1, :]
     centred = prod - rows_ref[...] * (col_sum / mock_count)
-    val = w_ref[...] * centred / (mock_count - 1)
+    val = centred * w_ref[...]
     o_ref[...] = jnp.where(keep_ref[...] > 0, val, jnp.float32(0.0)).astype(o_ref.dtype)
 
 
@@ -31,8 +31,8 @@
         pl.BlockSpec((fb, k), lambda j, off: (0, 0)),
         pl.BlockSpec((k, TILE_N), lambda j, off: (0, j)),
         pl.BlockSpec((fb, 1), lambda j, off: (0, 0)),
-        pl.BlockSpec((1, TILE_N), lambda j, off: (0, off[0] * tiles + j)),
-        pl.BlockSpec((1, TILE_N), lambda j, off: (0, off[0] * tiles + j)),
+        pl.BlockSpec((1, TILE_N), lambda j, off: (0, off[0] + j)),
+        pl.BlockSpec((1, TILE_N), lambda j, off: (0, off[0] + j)),
     ]
     args = [offset, own_t, panels_half, row_sums, weight_cols, keep_cols]
     aliases = {}
@@ -44,7 +44,7 @@
         num_scalar_prefetch=1,
         grid=(tiles,),
         in_specs=in_specs,
-        out_specs=pl.BlockSpec((fb, TILE_N), lambda j, off: (0, off[0] * tiles + j)),
+        out_specs=pl.BlockSpec((fb, TILE_N), lambda j, off: (0, off[0] + j)),
     )
     return pl.pallas_call(
         functools.partial(tile_kernel, k),
@@ -80,8 +80,11 @@
     local = local.reshape(m * ncore, n // ncore)
     sent = lax.all_to_all(local, ("y", "core"), split_axis=0, concat_axis=0, tiled=True)
     part = jnp.sum(sent.reshape(ny * ncore, m // ny, n // ncore), axis=0, dtype=sent.dtype)
-    own_half = lax.all_gather(part, ("col", "y"), axis=0, tiled=True)
-    other_half = lax.ppermute(own_half, "core", [(0, 1), (1, 0)])
+    quarter = part.shape[1] // 2
+    own_a = lax.all_gather(part[:, :quarter], ("col", "y"), axis=0, tiled=True)
+    own_b = lax.all_gather(part[:, quarter:], ("col", "y"), axis=0, tiled=True)
+    other_a = lax.ppermute(own_a, "core", [(0, 1), (1, 0)])
+    other_b = lax.ppermute(own_b, "core", [(0, 1), (1, 0)])
 
     own_block = lax.all_to_all(mock_maps, "col", split_axis=1, concat_axis=0, tiled=True)
     row_sums = jnp.sum(own_block, axis=0, dtype=jnp.float32)[:, None]
@@ -92,15 +95,20 @@
         ),
         axis=1,
     )
-    weight_cols = jnp.repeat(weights, block_width)[None, :]
+    mock_count = own_block.shape[0]
+    weight_cols = jnp.repeat(weights / (mock_count - 1), block_width)[None, :]
     keep_cols = jnp.repeat(kept_tiles[0], block_width)[None, :]
     own_t = own_block.T
-    first = half_tiles(
-        core.astype(jnp.int32).reshape(1), own_t, own_half, row_sums, weight_cols, keep_cols
+    step = own_a.shape[1] // TILE_N
+    mine = core.astype(jnp.int32) * 2 * step
+    theirs = (1 - core).astype(jnp.int32) * 2 * step
+    out = half_tiles(mine.reshape(1), own_t, own_a, row_sums, weight_cols, keep_cols)
+    out = half_tiles(
+        (mine + step).reshape(1), own_t, own_b, row_sums, weight_cols, keep_cols, prev=out
     )
+    out = half_tiles(theirs.reshape(1), own_t, other_a, row_sums, weight_cols, keep_cols, prev=out)
     return half_tiles(
-        (1 - core).astype(jnp.int32).reshape(1),
-        own_t, other_half, row_sums, weight_cols, keep_cols, prev=first,
+        (theirs + step).reshape(1), own_t, other_b, row_sums, weight_cols, keep_cols, prev=out
     )
 
 

time: 194 us -> 232 us (1.20)
  waiting for transfers between devices: 110 us -> 140 us
  starting transfers between devices: 6.5 us -> 11.5 us
    all_gather x1 -> x2, waiting for transfers between devices: 69.5 us -> 139 us  [the longest x1 73.8 us: device_body(): own_a = lax.all_gather(part[:, :quarter], ('col', 'y'), axis=0, tiled=True)]
    all_to_all x1, waiting for transfers between devices: 40.3 us -> 0.01 us  [device_body(): lax.all_to_all(mock_maps, 'col', split_axis=1, concat_axis=0, tiled=True)]
    all_to_all x1, starting transfers between devices: 4.35 us -> 7.73 us  [device_body(): lax.all_to_all(mock_maps, 'col', split_axis=1, concat_axis=0, tiled=True)]
    pallas_call x2 -> x4, Pallas kernels: 31.7 us -> 33.2 us  [half_tiles(): pl.pallas_call(functools.partial(tile_kernel, k), grid_spec=grid_spec, ou...]
  transfers between devices with their start and end apart: 3 -> 5, of which waited for: 2 -> 2; matrix products, arithmetic and copies ran while one was open for 3% -> 3% of each run, Pallas kernels for 8% -> 11%
where the time goes in v6:
time: 232 us
  waiting for transfers between devices  140 us (60%)
  Pallas kernels  33.2 us (14%)
  blocking collectives  16.7 us (7%)
  between operations  16.1 us (7%)
  starting transfers between devices  11.5 us (5%)
  local copies, waits for them, and re-layouts  11.2 us (5%)
  other arithmetic  3.92 us (2%)
    all_gather x1, waiting for transfers between devices, device_body(): own_a = lax.all_gather(part[:, :quarter], ('col', 'y'), axis=0, tiled=True)  73.8 us
    all_gather x1, waiting for transfers between devices, device_body(): own_b = lax.all_gather(part[:, quarter:], ('col', 'y'), axis=0, tiled=True)  65 us
    pallas_call x4, Pallas kernels, half_tiles(): pl.pallas_call(functools.partial(tile_kernel, k), grid_spec=grid_spec, ou...  33.2 us
    all_to_all x1, blocking collectives, device_body(): lax.all_to_all(local, ('y', 'core'), split_axis=0, concat_axis=0, tiled=T...  16.7 us
    all_to_all x1, starting transfers between devices, device_body(): lax.all_to_all(mock_maps, 'col', split_axis=1, concat_axis=0, tiled=True)  7.73 us
    all_to_all x2, local copies, waits for them, and re-layouts, device_body(): lax.all_to_all(mock_maps, 'col', split_axis=1, concat_axis=0, tiled=True)  4.75 us
  transfers between devices with their start and end apart: 5, of which 2 were waited for; matrix products, arithmetic and copies ran while one was open for 3% of the time, Pallas kernels for 11%

profile of v6, /device:TPU:1, one launch (start us, length us, event | category | flops | bytes accessed | tf_op | source)
XLA Modules:
  0.0 232.1 jit_solution(3185732281689215681)
XLA Ops:
  6.5 1.4 fusion.1
  10.5 1.3 dynamic-slice_select_fusion.3
  11.8 0.0 copy-start.4
  11.9 1.3 reshape.27
  13.2 1.2 copy.31
  14.3 16.7 %all_to_all.28 = bf16[8,16,2560]{2,1,0:T(8,128)(2,1)S(1)} all-to-all(bf16[8,16,2560]{2,1,0:T(8,128)(2,1)S(1)} %bitcast.46), channel_id=1, replica_groups=mesh['y'=4,'core'=2,'col'=16] {'y','core'}, dimensions={0} | all-to-all | bytes 1310720 | tf_op jit(solution)/shard_map/all_to_all | solution.py:81
  31.0 0.1 reduce_sum.27
  31.1 0.6 fusion
  31.7 0.0 all-gather.5.cloned.1.call-update
  31.7 0.0 all-gather.3.cloned.1.call-start
  31.8 0.7 all-gather.3.cloned.1.call-update
  32.5 1.8 copy.40
  34.3 7.7 %all-to-all-start = ((bf16[64,16,1280]{2,0,1:T(8,128)(2,1)}), bf16[64,16,1280]{2,0,1:T(8,128)(2,1)S(1)}, u32[]{:S(2)}, u32[]{:S(2)}) async-start(bf16[64,16,1280]{2,0,1:T(8,128)(2,1)} %bitcast.43), calls=%async_computation | async-start | bytes 5242880 | tf_op jit(solution)/shard_map/all_to_all | solution.py:89
  42.0 73.8 %all-gather.5.cloned.1.call-done.b_ref = bf16[1024,1280]{1,0:T(8,128)(2,1)} async-done(((bf16[16,1280]{1,0:T(8,128)(2,1)}), bf16[1024,1280]{1,0:T(8,128)(2,1)}) %all-gather.5.cloned.1.call-update) | async-done | bytes 2621456 | tf_op jit(solution)/shard_map/all_gather | solution.py:84
  115.8 1.8 collective-permute-start.1
  117.7 65.0 %all-gather.3.cloned.1.call-done.b_ref = bf16[1024,1280]{1,0:T(8,128)(2,1)} async-done(((bf16[16,1280]{1,0:T(8,128)(2,1)}), bf16[1024,1280]{1,0:T(8,128)(2,1)}) %all-gather.3.cloned.1.call-update) | async-done | bytes 2621456 | tf_op jit(solution)/shard_map/all_gather | solution.py:85
  182.6 1.8 collective-permute-start
  184.5 0.2 select_reduce_fusion
  184.7 0.1 broadcast_bitcast_fusion.1
  184.8 0.1 broadcast_bitcast_fusion
  184.9 0.0 all-to-all-done
  184.9 0.0 copy-start.3
  184.9 1.5 copy-done.3
  186.4 3.0 %copy.30 = bf16[1024,1280]{0,1:T(8,128)(2,1)S(1)} copy(bf16[1024,1280]{1,0:T(8,128)(2,1)} %bitcast.42) | data formatting | bytes 5242880 | tf_op jit(solution)/shard_map/all_to_all | solution.py:89
  189.4 2.3 convert_reduce_fusion
  191.7 0.2 broadcast_in_dim.28.rows_ref
  192.0 7.8 %shard_map.55.rest_0_ = bf16[1280,5120]{1,0:T(8,128)(2,1)} custom-call(s32[1]{0:T(128)} %bitcast.14.off_ref, bf16[1280,1024]{1,0:T(8,128)(2,1)S(1)} %bitcast.30, bf16[1024,1280]{1,0:T(8,128)(2,1)S(1)} %copy-done.2, f32[1280,1]{1,0:T(8,128)S(1)} %broadcast_in_dim.28.rows_ref, f32[1,5120]{1,0:T(1,128)S(1)} %bitcast.34, s32[1,5120]{1,0:T(1,128)S(1)} %bitcast.38), custom_call_target="tpu_custom_call" | custom-call | flops 3355443200 | bytes 8519680 | tf_op jit(solution)/shard_map/pallas_call | solution.py:49
  199.8 7.8 %shard_map.56.rest_0_ = bf16[1280,5120]{1,0:T(8,128)(2,1)} custom-call(s32[1]{0:T(128)} %bitcast.13.off_ref, bf16[1280,1024]{1,0:T(8,128)(2,1)S(1)} %bitcast.31, bf16[1024,1280]{1,0:T(8,128)(2,1)S(1)} %copy-done.1, f32[1280,1]{1,0:T(8,128)S(1)} %broadcast_in_dim.28.rows_ref, f32[1,5120]{1,0:T(1,128)S(1)} %bitcast.35, ...), custom_call_target="tpu_custom_call", output_to_operand_aliasing={{}: (6, {})} | custom-call | flops 3355443200 | bytes 8519680 | tf_op jit(solution)/shard_map/pallas_call | solution.py:49
  207.5 0.0 collective-permute-done.1.b_ref
  207.5 8.8 %shard_map.57.rest_0_ = bf16[1280,5120]{1,0:T(8,128)(2,1)} custom-call(s32[1]{0:T(128)} %bitcast.12.off_ref, bf16[1280,1024]{1,0:T(8,128)(2,1)S(1)} %bitcast.32, bf16[1024,1280]{1,0:T(8,128)(2,1)} %collective-permute-done.1.b_ref, f32[1280,1]{1,0:T(8,128)S(1)} %broadcast_in_dim.28.rows_ref, f32[1,5120]{1,0:T(1,128)S(1)} %bitcast.36, ...), custom_call_target="tpu_custom_call", output_to_operand_aliasing={{}: (6, {})} | custom-call | flops 3355443200 | bytes 8519680 | tf_op jit(solution)/shard_map/pallas_call | solution.py:49
  216.4 0.0 collective-permute-done.b_ref
  216.4 8.8 %shard_map.58 = bf16[1280,5120]{1,0:T(8,128)(2,1)} custom-call(s32[1]{0:T(128)} %bitcast.off_ref, bf16[1280,1024]{1,0:T(8,128)(2,1)S(1)} %bitcast.33, bf16[1024,1280]{1,0:T(8,128)(2,1)} %collective-permute-done.b_ref, f32[1280,1]{1,0:T(8,128)S(1)} %broadcast_in_dim.28.rows_ref, f32[1,5120]{1,0:T(1,128)S(1)} %bitcast.37, ...), custom_call_target="tpu_custom_call", output_to_operand_aliasing={{}: (6, {})} | custom-call | flops 3355443200 | bytes 8519680 | tf_op jit(solution)/shard_map/pallas_call | solution.py:49
  (16 shorter events, 0.1 us)
Async XLA Ops:
  6.5 178.2 %copy-start = (s32[1,4]{1,0:T(1,128)S(1)}, s32[1,4]{1,0:T(1,128)}, u32[]{:S(2)}) copy-start(s32[1,4]{1,0:T(1,128)} %param.7) | copy-start | bytes 52
  6.5 109.3 %all-gather.5.cloned.1.call-start = ((), (), s32[]{:S(2)}) async-start(), calls=%async_computation.3 | async-start | bytes 2662400 | tf_op jit(solution)/shard_map/all_gather | solution.py:84
  11.8 20.6 %copy-start.4 = (bf16[64,20480]{1,0:T(8,128)(2,1)S(1)}, bf16[64,20480]{1,0:T(8,128)(2,1)}, u32[]{:S(2)}) copy-start(bf16[64,20480]{1,0:T(8,128)(2,1)} %param.5) | copy-start | bytes 7864324
  31.7 150.9 %all-gather.3.cloned.1.call-start = ((), (), s32[]{:S(2)}) async-start(), calls=%async_computation.2 | async-start | bytes 2662400 | tf_op jit(solution)/shard_map/all_gather | solution.py:85
  34.3 150.2 %copy-start.5 = (f32[4]{0:T(128)S(1)}, f32[4]{0:T(128)}, u32[]{:S(2)}) copy-start(f32[4]{0:T(128)} %param.9) | copy-start | bytes 52
  34.3 150.2 %copy-start.6 = (s32[1,4]{1,0:T(1,128)S(1)}, s32[1,4]{1,0:T(1,128)}, u32[]{:S(2)}) copy-start(s32[1,4]{1,0:T(1,128)} %param.8) | copy-start | bytes 52
  34.3 150.6 %all-to-all-start = ((bf16[64,16,1280]{2,0,1:T(8,128)(2,1)}), bf16[64,16,1280]{2,0,1:T(8,128)(2,1)S(1)}, u32[]{:S(2)}, u32[]{:S(2)}) async-start(bf16[64,16,1280]{2,0,1:T(8,128)(2,1)} %bitcast.43), calls=%async_computation | async-start | bytes 5242880 | tf_op jit(solution)/shard_map/all_to_all | solution.py:89
  115.8 91.7 %collective-permute-start.1 = (bf16[1024,1280]{1,0:T(8,128)(2,1)}, bf16[1024,1280]{1,0:T(8,128)(2,1)}, u32[]{:S(2)}, u32[]{:S(2)}) collective-permute-start(bf16[1024,1280]{1,0:T(8,128)(2,1)} %all-gather.5.cloned.1.call-done.b_ref), channel_id=1, source_target_pairs={{0,16},{16,0},{1,17},{17,1},{2,18},{18,2},{3,19},{19,3},{4,20},{20... | collective-permute-start | bytes 7864328 | tf_op jit(solution)/shard_map/ppermute | solution.py:86
  182.6 33.7 %collective-permute-start = (bf16[1024,1280]{1,0:T(8,128)(2,1)}, bf16[1024,1280]{1,0:T(8,128)(2,1)}, u32[]{:S(2)}, u32[]{:S(2)}) collective-permute-start(bf16[1024,1280]{1,0:T(8,128)(2,1)} %all-gather.3.cloned.1.call-done.b_ref), channel_id=1, source_target_pairs={{0,16},{16,0},{1,17},{17,1},{2,18},{18,2},{3,19},{19,3},{4,20},{20... | collective-permute-start | bytes 7864328 | tf_op jit(solution)/shard_map/ppermute | solution.py:87
  184.9 1.5 copy-start.3
  189.4 2.6 %copy-start.2 = (bf16[1024,1280]{1,0:T(8,128)(2,1)S(1)}, bf16[1024,1280]{1,0:T(8,128)(2,1)}, u32[]{:S(2)}) copy-start(bf16[1024,1280]{1,0:T(8,128)(2,1)} %all-gather.5.cloned.1.call-done.b_ref) | copy-start | bytes 7864324
  192.0 7.8 %copy-start.1 = (bf16[1024,1280]{1,0:T(8,128)(2,1)S(1)}, bf16[1024,1280]{1,0:T(8,128)(2,1)}, u32[]{:S(2)}) copy-start(bf16[1024,1280]{1,0:T(8,128)(2,1)} %all-gather.3.cloned.1.call-done.b_ref) | copy-start | bytes 7864324
Sparse Core Ops, SparseCore 0:
  31.9 83.9 all-gather.4
  118.7 63.9 all-gather.2

commit v7 on v5

--- a/solution.py
+++ b/solution.py
@@ -19,7 +19,7 @@
     ones = jnp.ones((8, b.shape[0]), b.dtype)
     col_sum = jnp.dot(ones, b, preferred_element_type=jnp.float32)[0:1, :]
     centred = prod - rows_ref[...] * (col_sum / mock_count)
-    val = w_ref[...] * centred / (mock_count - 1)
+    val = centred * w_ref[...]
     o_ref[...] = jnp.where(keep_ref[...] > 0, val, jnp.float32(0.0)).astype(o_ref.dtype)
 
 
@@ -80,7 +80,8 @@
     local = local.reshape(m * ncore, n // ncore)
     sent = lax.all_to_all(local, ("y", "core"), split_axis=0, concat_axis=0, tiled=True)
     part = jnp.sum(sent.reshape(ny * ncore, m // ny, n // ncore), axis=0, dtype=sent.dtype)
-    own_half = lax.all_gather(part, ("col", "y"), axis=0, tiled=True)
+    part = lax.all_gather(part, "y", axis=0, tiled=True)
+    own_half = lax.all_gather(part, "col", axis=0, tiled=True)
     other_half = lax.ppermute(own_half, "core", [(0, 1), (1, 0)])
 
     own_block = lax.all_to_all(mock_maps, "col", split_axis=1, concat_axis=0, tiled=True)
@@ -92,7 +93,8 @@
         ),
         axis=1,
     )
-    weight_cols = jnp.repeat(weights, block_width)[None, :]
+    mock_count = own_block.shape[0]
+    weight_cols = jnp.repeat(weights / (mock_count - 1), block_width)[None, :]
     keep_cols = jnp.repeat(kept_tiles[0], block_width)[None, :]
     own_t = own_block.T
     first = half_tiles(

time: 194 us -> 191 us (0.985)
  blocking collectives: 16.7 us -> 26.9 us
  waiting for transfers between devices: 110 us -> 101 us
  Pallas kernels: 31.7 us -> 28.5 us
    all_gather x0 -> x1, blocking collectives: none -> 10.2 us  [device_body(): part = lax.all_gather(part, 'y', axis=0, tiled=True)]
    all_gather x1, waiting for transfers between devices: 69.5 us -> 60.4 us  [device_body(): own_half = lax.all_gather(part, 'col', axis=0, tiled=True)]
    pallas_call x2, Pallas kernels: 31.7 us -> 28.5 us  [half_tiles(): pl.pallas_call(functools.partial(tile_kernel, k), grid_spec=grid_spec, ou...]
where the time goes in v7:
time: 191 us; the launch traced here: 190 us
  waiting for transfers between devices  101 us (53%)
  Pallas kernels  28.5 us (15%)
  blocking collectives  26.9 us (14%)
  between operations  16.1 us (8%)
  local copies, waits for them, and re-layouts  9.9 us (5%)
  starting transfers between devices  5.95 us (3%)
  other arithmetic  2.07 us (1%)
    all_gather x1, waiting for transfers between devices, device_body(): own_half = lax.all_gather(part, 'col', axis=0, tiled=True)  60.4 us
    all_to_all x1, waiting for transfers between devices, device_body(): lax.all_to_all(mock_maps, 'col', split_axis=1, concat_axis=0, tiled=True)  40.3 us
    pallas_call x2, Pallas kernels, half_tiles(): pl.pallas_call(functools.partial(tile_kernel, k), grid_spec=grid_spec, ou...  28.5 us
    all_to_all x1, blocking collectives, device_body(): lax.all_to_all(local, ('y', 'core'), split_axis=0, concat_axis=0, tiled=T...  16.7 us
    all_gather x1, blocking collectives, device_body(): part = lax.all_gather(part, 'y', axis=0, tiled=True)  10.2 us
    all_to_all x1, starting transfers between devices, device_body(): lax.all_to_all(mock_maps, 'col', split_axis=1, concat_axis=0, tiled=True)  5.11 us
    all_to_all x2, local copies, waits for them, and re-layouts, device_body(): lax.all_to_all(mock_maps, 'col', split_axis=1, concat_axis=0, tiled=True)  4.75 us
  transfers between devices with their start and end apart: 3, of which 2 were waited for; matrix products, arithmetic and copies ran while one was open for 3% of the time, Pallas kernels for 8%

profile of v7, /device:TPU:1, one launch (start us, length us, event | category | flops | bytes accessed | tf_op | source)
XLA Modules:
  0.0 190.2 jit_solution(15570699068337417611)
XLA Ops:
  6.5 0.0 copy-start
  6.5 0.0 all-gather.2.cloned.1.call-start
  6.5 1.5 fusion
  10.6 1.3 dynamic-slice_select_fusion.3
  11.9 0.0 copy-start.2
  11.9 1.3 reshape.21
  13.2 1.2 copy.23
  14.4 16.7 %all_to_all.28 = bf16[8,16,2560]{2,1,0:T(8,128)(2,1)S(1)} all-to-all(bf16[8,16,2560]{2,1,0:T(8,128)(2,1)S(1)} %bitcast.38), channel_id=1, replica_groups=mesh['y'=4,'core'=2,'col'=16] {'y','core'}, dimensions={0} | all-to-all | bytes 1310720 | tf_op jit(solution)/shard_map/all_to_all | solution.py:81
  31.0 0.1 reduce_sum.27
  31.1 10.2 %all_gather.6 = bf16[64,2560]{1,0:T(8,128)(2,1)} all-gather(bf16[16,2560]{1,0:T(8,128)(2,1)S(1)} %reduce_sum.27), channel_id=1, replica_groups=mesh['y'=4,'core'=2,'col'=16] {'y'}, dimensions={0}, use_global_device_ids=true | all-gather | bytes 409600 | tf_op jit(solution)/shard_map/all_gather | solution.py:83
  41.4 0.0 all-gather.2.cloned.1.call-update
  41.4 60.4 %all-gather.2.cloned.1.call-done.b_ref = bf16[1024,2560]{1,0:T(8,128)(2,1)} async-done(((bf16[64,2560]{1,0:T(8,128)(2,1)}), bf16[1024,2560]{1,0:T(8,128)(2,1)}) %all-gather.2.cloned.1.call-update) | async-done | bytes 5242896 | tf_op jit(solution)/shard_map/all_gather | solution.py:84
  101.9 0.8 collective-permute-start
  102.7 0.0 copy-done.2
  102.7 1.8 copy.30
  104.5 0.0 copy-start.4
  104.5 5.1 %all-to-all-start = ((bf16[64,16,1280]{2,0,1:T(8,128)(2,1)}), bf16[64,16,1280]{2,0,1:T(8,128)(2,1)S(1)}, u32[]{:S(2)}, u32[]{:S(2)}) async-start(bf16[64,16,1280]{2,0,1:T(8,128)(2,1)} %bitcast.35), calls=%async_computation | async-start | bytes 5242880 | tf_op jit(solution)/shard_map/all_to_all | solution.py:87
  109.6 0.0 copy-done.3
  109.6 0.0 copy-done.4
  109.6 0.2 select_reduce_fusion
  109.8 0.1 broadcast_bitcast_fusion.1
  109.9 0.0 copy-done
  109.9 0.1 broadcast_bitcast_fusion
  110.0 40.3 %all-to-all-done = bf16[64,16,1280]{2,0,1:T(8,128)(2,1)S(1)} async-done(((bf16[64,16,1280]{2,0,1:T(8,128)(2,1)}), bf16[64,16,1280]{2,0,1:T(8,128)(2,1)S(1)}, u32[]{:S(2)}, u32[]{:S(2)}) %all-to-all-start) | async-done | bytes 2621472 | tf_op jit(solution)/shard_map/all_to_all | solution.py:87
  150.3 0.0 copy-start.1
  150.3 0.5 convert_reduce_fusion
  150.8 0.2 broadcast_in_dim.28.rows_ref
  151.0 0.8 copy-done.1
  151.8 3.0 %copy.22 = bf16[1024,1280]{0,1:T(8,128)(2,1)S(1)} copy(bf16[1024,1280]{1,0:T(8,128)(2,1)} %bitcast.34) | data formatting | bytes 5242880 | tf_op jit(solution)/shard_map/all_to_all | solution.py:87
  154.8 14.3 %shard_map.55.rest_0_ = bf16[1280,5120]{1,0:T(8,128)(2,1)} custom-call(s32[1]{0:T(128)} %bitcast.12.off_ref, bf16[1280,1024]{1,0:T(8,128)(2,1)S(1)} %bitcast.28, bf16[1024,2560]{1,0:T(8,128)(2,1)} %all-gather.2.cloned.1.call-done.b_ref, f32[1280,1]{1,0:T(8,128)S(1)} %broadcast_in_dim.28.rows_ref, f32[1,5120]{1,0:T(1,128)S(1)} %bitcast.30, s32[1,5120]{1,0:T(1,128)S(1)} %bitcast.32), custom_call_target="tpu_custom_call" | custom-call | flops 6710886400 | bytes 14417920 | tf_op jit(solution)/shard_map/pallas_call | solution.py:49
  169.1 0.0 collective-permute-done.b_ref
  169.1 14.3 %shard_map.56 = bf16[1280,5120]{1,0:T(8,128)(2,1)} custom-call(s32[1]{0:T(128)} %bitcast.off_ref, bf16[1280,1024]{1,0:T(8,128)(2,1)S(1)} %bitcast.29, bf16[1024,2560]{1,0:T(8,128)(2,1)} %collective-permute-done.b_ref, f32[1280,1]{1,0:T(8,128)S(1)} %broadcast_in_dim.28.rows_ref, f32[1,5120]{1,0:T(1,128)S(1)} %bitcast.31, ...), custom_call_target="tpu_custom_call", output_to_operand_aliasing={{}: (6, {})} | custom-call | flops 6710886400 | bytes 14417920 | tf_op jit(solution)/shard_map/pallas_call | solution.py:49
  (5 shorter events, 0.1 us)
Async XLA Ops:
  6.5 103.4 %copy-start = (s32[1,4]{1,0:T(1,128)S(1)}, s32[1,4]{1,0:T(1,128)}, u32[]{:S(2)}) copy-start(s32[1,4]{1,0:T(1,128)} %param.7) | copy-start | bytes 52
  6.5 95.3 %all-gather.2.cloned.1.call-start = ((), (), s32[]{:S(2)}) async-start(), calls=%async_computation.2 | async-start | bytes 5570560 | tf_op jit(solution)/shard_map/all_gather | solution.py:84
  11.9 90.8 %copy-start.2 = (bf16[64,20480]{1,0:T(8,128)(2,1)S(1)}, bf16[64,20480]{1,0:T(8,128)(2,1)}, u32[]{:S(2)}) copy-start(bf16[64,20480]{1,0:T(8,128)(2,1)} %param.5) | copy-start | bytes 7864324
  101.9 67.2 %collective-permute-start = (bf16[1024,2560]{1,0:T(8,128)(2,1)}, bf16[1024,2560]{1,0:T(8,128)(2,1)}, u32[]{:S(2)}, u32[]{:S(2)}) collective-permute-start(bf16[1024,2560]{1,0:T(8,128)(2,1)} %all-gather.2.cloned.1.call-done.b_ref), channel_id=1, source_target_pairs={{0,16},{16,0},{1,17},{17,1},{2,18},{18,2},{3,19},{19,3},{4,20},{20... | collective-permute-start | bytes 15728648 | tf_op jit(solution)/shard_map/ppermute | solution.py:85
  104.5 5.1 %copy-start.3 = (f32[4]{0:T(128)S(1)}, f32[4]{0:T(128)}, u32[]{:S(2)}) copy-start(f32[4]{0:T(128)} %param.9) | copy-start | bytes 52
  104.5 5.1 %copy-start.4 = (s32[1,4]{1,0:T(1,128)S(1)}, s32[1,4]{1,0:T(1,128)}, u32[]{:S(2)}) copy-start(s32[1,4]{1,0:T(1,128)} %param.8) | copy-start | bytes 52
  104.5 45.9 %all-to-all-start = ((bf16[64,16,1280]{2,0,1:T(8,128)(2,1)}), bf16[64,16,1280]{2,0,1:T(8,128)(2,1)S(1)}, u32[]{:S(2)}, u32[]{:S(2)}) async-start(bf16[64,16,1280]{2,0,1:T(8,128)(2,1)} %bitcast.35), calls=%async_computation | async-start | bytes 5242880 | tf_op jit(solution)/shard_map/all_to_all | solution.py:87
  150.3 1.5 copy-start.1
Sparse Core Ops, SparseCore 0:
  41.5 60.2 all-gather.1

commit v8 on v7

--- a/solution.py
+++ b/solution.py
@@ -9,7 +9,7 @@
 from jax.sharding import PartitionSpec as P
 
 WINDOW = 4
-TILE_N = 512
+TILE_N = 1280
 
 
 def tile_kernel(mock_count, off_ref, a_ref, b_ref, rows_ref, w_ref, keep_ref, *rest):
@@ -80,8 +80,7 @@
     local = local.reshape(m * ncore, n // ncore)
     sent = lax.all_to_all(local, ("y", "core"), split_axis=0, concat_axis=0, tiled=True)
     part = jnp.sum(sent.reshape(ny * ncore, m // ny, n // ncore), axis=0, dtype=sent.dtype)
-    part = lax.all_gather(part, "y", axis=0, tiled=True)
-    own_half = lax.all_gather(part, "col", axis=0, tiled=True)
+    own_half = lax.all_gather(part, ("col", "y"), axis=0, tiled=True)
     other_half = lax.ppermute(own_half, "core", [(0, 1), (1, 0)])
 
     own_block = lax.all_to_all(mock_maps, "col", split_axis=1, concat_axis=0, tiled=True)

time: 191 us -> 191 us (level)
  blocking collectives: 26.9 us -> 16.7 us
  waiting for transfers between devices: 101 us -> 110 us
    all_gather x1 -> x0, blocking collectives: 10.2 us -> none  [device_body(): part = lax.all_gather(part, 'y', axis=0, tiled=True)]
    all_gather x1, waiting for transfers between devices: 60.4 us -> 69.5 us  [device_body(): own_half = lax.all_gather(part, ('col', 'y'), axis=0, tiled=True)]
where the time goes in v8:
time: 191 us; the launch traced here: 190 us
  waiting for transfers between devices  110 us (58%)
  Pallas kernels  28.7 us (15%)
  blocking collectives  16.7 us (9%)
  between operations  16.1 us (8%)
  local copies, waits for them, and re-layouts  9.9 us (5%)
  starting transfers between devices  6.5 us (3%)
  other arithmetic  2.7 us (1%)
    all_gather x1, waiting for transfers between devices, device_body(): own_half = lax.all_gather(part, ('col', 'y'), axis=0, tiled=True)  69.5 us
    all_to_all x1, waiting for transfers between devices, device_body(): lax.all_to_all(mock_maps, 'col', split_axis=1, concat_axis=0, tiled=True)  40.3 us
    pallas_call x2, Pallas kernels, half_tiles(): pl.pallas_call(functools.partial(tile_kernel, k), grid_spec=grid_spec, ou...  28.7 us
    all_to_all x1, blocking collectives, device_body(): lax.all_to_all(local, ('y', 'core'), split_axis=0, concat_axis=0, tiled=T...  16.7 us
    all_to_all x2, local copies, waits for them, and re-layouts, device_body(): lax.all_to_all(mock_maps, 'col', split_axis=1, concat_axis=0, tiled=True)  4.75 us
    all_to_all x1, starting transfers between devices, device_body(): lax.all_to_all(mock_maps, 'col', split_axis=1, concat_axis=0, tiled=True)  4.35 us
  transfers between devices with their start and end apart: 3, of which 2 were waited for; matrix products, arithmetic and copies ran while one was open for 3% of the time, Pallas kernels for 8%

profile of v8, /device:TPU:1, one launch (start us, length us, event | category | flops | bytes accessed | tf_op | source)
XLA Modules:
  0.0 190.4 jit_solution(14495669085988296859)
XLA Ops:
  6.5 0.0 copy-start
  6.5 0.0 all-gather.2.cloned.1.call-start
  6.5 1.5 fusion
  10.6 1.3 dynamic-slice_select_fusion.3
  11.9 0.0 copy-start.2
  11.9 1.3 reshape.21
  13.2 1.2 copy.23
  14.4 16.7 %all_to_all.28 = bf16[8,16,2560]{2,1,0:T(8,128)(2,1)S(1)} all-to-all(bf16[8,16,2560]{2,1,0:T(8,128)(2,1)S(1)} %bitcast.38), channel_id=1, replica_groups=mesh['y'=4,'core'=2,'col'=16] {'y','core'}, dimensions={0} | all-to-all | bytes 1310720 | tf_op jit(solution)/shard_map/all_to_all | solution.py:81
  31.0 0.7 reduce_sum.27
  31.8 0.0 all-gather.2.cloned.1.call-update
  31.8 69.5 %all-gather.2.cloned.1.call-done.b_ref = bf16[1024,2560]{1,0:T(8,128)(2,1)} async-done(((bf16[16,2560]{1,0:T(8,128)(2,1)}), bf16[1024,2560]{1,0:T(8,128)(2,1)}) %all-gather.2.cloned.1.call-update) | async-done | bytes 5242896 | tf_op jit(solution)/shard_map/all_gather | solution.py:83
  101.3 2.1 %collective-permute-start = (bf16[1024,2560]{1,0:T(8,128)(2,1)}, bf16[1024,2560]{1,0:T(8,128)(2,1)}, u32[]{:S(2)}, u32[]{:S(2)}) collective-permute-start(bf16[1024,2560]{1,0:T(8,128)(2,1)} %all-gather.2.cloned.1.call-done.b_ref), channel_id=1, source_target_pairs={{0,16},{16,0},{1,17},{17,1},{2,18},{18,2},{3,19},{19,3},{4,20},{20... | collective-permute-start | bytes 15728648 | tf_op jit(solution)/shard_map/ppermute | solution.py:84
  103.5 0.0 copy-done.2
  103.5 1.8 copy.30
  105.2 0.0 copy-start.3
  105.2 0.0 copy-start.4
  105.2 4.4 %all-to-all-start = ((bf16[64,16,1280]{2,0,1:T(8,128)(2,1)}), bf16[64,16,1280]{2,0,1:T(8,128)(2,1)S(1)}, u32[]{:S(2)}, u32[]{:S(2)}) async-start(bf16[64,16,1280]{2,0,1:T(8,128)(2,1)} %bitcast.35), calls=%async_computation | async-start | bytes 5242880 | tf_op jit(solution)/shard_map/all_to_all | solution.py:86
  109.6 0.0 copy-done.3
  109.6 0.0 copy-done.4
  109.6 0.2 select_reduce_fusion
  109.8 0.1 broadcast_bitcast_fusion.1
  109.9 0.0 copy-done
  109.9 0.1 broadcast_bitcast_fusion
  110.0 40.3 %all-to-all-done = bf16[64,16,1280]{2,0,1:T(8,128)(2,1)S(1)} async-done(((bf16[64,16,1280]{2,0,1:T(8,128)(2,1)}), bf16[64,16,1280]{2,0,1:T(8,128)(2,1)S(1)}, u32[]{:S(2)}, u32[]{:S(2)}) %all-to-all-start) | async-done | bytes 2621472 | tf_op jit(solution)/shard_map/all_to_all | solution.py:86
  150.3 0.0 copy-start.1
  150.3 0.5 convert_reduce_fusion
  150.8 0.2 broadcast_in_dim.28.rows_ref
  151.0 0.8 copy-done.1
  151.8 3.0 %copy.22 = bf16[1024,1280]{0,1:T(8,128)(2,1)S(1)} copy(bf16[1024,1280]{1,0:T(8,128)(2,1)} %bitcast.34) | data formatting | bytes 5242880 | tf_op jit(solution)/shard_map/all_to_all | solution.py:86
  154.8 14.4 %shard_map.55.rest_0_ = bf16[1280,5120]{1,0:T(8,128)(2,1)} custom-call(s32[1]{0:T(128)} %bitcast.12.off_ref, bf16[1280,1024]{1,0:T(8,128)(2,1)S(1)} %bitcast.28, bf16[1024,2560]{1,0:T(8,128)(2,1)} %all-gather.2.cloned.1.call-done.b_ref, f32[1280,1]{1,0:T(8,128)S(1)} %broadcast_in_dim.28.rows_ref, f32[1,5120]{1,0:T(1,128)S(1)} %bitcast.30, s32[1,5120]{1,0:T(1,128)S(1)} %bitcast.32), custom_call_target="tpu_custom_call" | custom-call | flops 6710886400 | bytes 14417920 | tf_op jit(solution)/shard_map/pallas_call | solution.py:49
  169.2 0.0 collective-permute-done.b_ref
  169.2 14.4 %shard_map.56 = bf16[1280,5120]{1,0:T(8,128)(2,1)} custom-call(s32[1]{0:T(128)} %bitcast.off_ref, bf16[1280,1024]{1,0:T(8,128)(2,1)S(1)} %bitcast.29, bf16[1024,2560]{1,0:T(8,128)(2,1)} %collective-permute-done.b_ref, f32[1280,1]{1,0:T(8,128)S(1)} %broadcast_in_dim.28.rows_ref, f32[1,5120]{1,0:T(1,128)S(1)} %bitcast.31, ...), custom_call_target="tpu_custom_call", output_to_operand_aliasing={{}: (6, {})} | custom-call | flops 6710886400 | bytes 14417920 | tf_op jit(solution)/shard_map/pallas_call | solution.py:49
  (4 shorter events, 0.1 us)
Async XLA Ops:
  6.5 103.4 %copy-start = (s32[1,4]{1,0:T(1,128)S(1)}, s32[1,4]{1,0:T(1,128)}, u32[]{:S(2)}) copy-start(s32[1,4]{1,0:T(1,128)} %param.7) | copy-start | bytes 52
  6.5 94.8 %all-gather.2.cloned.1.call-start = ((), (), s32[]{:S(2)}) async-start(), calls=%async_computation.2 | async-start | bytes 5324800 | tf_op jit(solution)/shard_map/all_gather | solution.py:83
  11.9 91.5 %copy-start.2 = (bf16[64,20480]{1,0:T(8,128)(2,1)S(1)}, bf16[64,20480]{1,0:T(8,128)(2,1)}, u32[]{:S(2)}) copy-start(bf16[64,20480]{1,0:T(8,128)(2,1)} %param.5) | copy-start | bytes 7864324
  101.3 67.9 %collective-permute-start = (bf16[1024,2560]{1,0:T(8,128)(2,1)}, bf16[1024,2560]{1,0:T(8,128)(2,1)}, u32[]{:S(2)}, u32[]{:S(2)}) collective-permute-start(bf16[1024,2560]{1,0:T(8,128)(2,1)} %all-gather.2.cloned.1.call-done.b_ref), channel_id=1, source_target_pairs={{0,16},{16,0},{1,17},{17,1},{2,18},{18,2},{3,19},{19,3},{4,20},{20... | collective-permute-start | bytes 15728648 | tf_op jit(solution)/shard_map/ppermute | solution.py:84
  105.2 4.4 %copy-start.3 = (f32[4]{0:T(128)S(1)}, f32[4]{0:T(128)}, u32[]{:S(2)}) copy-start(f32[4]{0:T(128)} %param.9) | copy-start | bytes 52
  105.2 4.4 %copy-start.4 = (s32[1,4]{1,0:T(1,128)S(1)}, s32[1,4]{1,0:T(1,128)}, u32[]{:S(2)}) copy-start(s32[1,4]{1,0:T(1,128)} %param.8) | copy-start | bytes 52
  105.2 45.1 %all-to-all-start = ((bf16[64,16,1280]{2,0,1:T(8,128)(2,1)}), bf16[64,16,1280]{2,0,1:T(8,128)(2,1)S(1)}, u32[]{:S(2)}, u32[]{:S(2)}) async-start(bf16[64,16,1280]{2,0,1:T(8,128)(2,1)} %bitcast.35), calls=%async_computation | async-start | bytes 5242880 | tf_op jit(solution)/shard_map/all_to_all | solution.py:86
  150.3 1.5 copy-start.1
Sparse Core Ops, SparseCore 0:
  31.9 69.3 all-gather.1

commit v9 on v8

--- a/solution.py
+++ b/solution.py
@@ -80,7 +80,7 @@
     local = local.reshape(m * ncore, n // ncore)
     sent = lax.all_to_all(local, ("y", "core"), split_axis=0, concat_axis=0, tiled=True)
     part = jnp.sum(sent.reshape(ny * ncore, m // ny, n // ncore), axis=0, dtype=sent.dtype)
-    own_half = lax.all_gather(part, ("col", "y"), axis=0, tiled=True)
+    own_half = lax.all_gather(part, ("y", "col"), axis=0, tiled=True)
     other_half = lax.ppermute(own_half, "core", [(0, 1), (1, 0)])
 
     own_block = lax.all_to_all(mock_maps, "col", split_axis=1, concat_axis=0, tiled=True)
@@ -95,7 +95,10 @@
     mock_count = own_block.shape[0]
     weight_cols = jnp.repeat(weights / (mock_count - 1), block_width)[None, :]
     keep_cols = jnp.repeat(kept_tiles[0], block_width)[None, :]
-    own_t = own_block.T
+    ncol = lax.axis_size("col")
+    fb = own_block.shape[1]
+    own_t = own_block.reshape(ncol, ny, mock_count // (ncol * ny), fb)
+    own_t = own_t.transpose(3, 1, 0, 2).reshape(fb, mock_count)
     first = half_tiles(
         core.astype(jnp.int32).reshape(1), own_t, own_half, row_sums, weight_cols, keep_cols
     )

time: 191 us -> 191 us (level)
    all_to_all x2 -> x1, local copies, waits for them, and re-layouts: 4.75 us -> 1.76 us  [device_body(): lax.all_to_all(mock_maps, 'col', split_axis=1, concat_axis=0, tiled=True)]
    reshape x0 -> x1, local copies, waits for them, and re-layouts: none -> 2.99 us  [device_body(): own_t = own_t.transpose(3, 1, 0, 2).reshape(fb, mock_count)]
  transfers between devices with their start and end apart: 3 -> 3, of which waited for: 2 -> 2; matrix products, arithmetic and copies ran while one was open for 3% -> 4% of each run, Pallas kernels for 8% -> 8%
where the time goes in v9:
time: 191 us
  waiting for transfers between devices  110 us (58%)
  Pallas kernels  28.7 us (15%)
  blocking collectives  16.7 us (9%)
  between operations  16 us (8%)
  local copies, waits for them, and re-layouts  10.8 us (6%)
  starting transfers between devices  6.5 us (3%)
  other arithmetic  2.7 us (1%)
    all_gather x1, waiting for transfers between devices, device_body(): own_half = lax.all_gather(part, ('y', 'col'), axis=0, tiled=True)  69.5 us
    all_to_all x1, waiting for transfers between devices, device_body(): lax.all_to_all(mock_maps, 'col', split_axis=1, concat_axis=0, tiled=True)  40.3 us
    pallas_call x2, Pallas kernels, half_tiles(): pl.pallas_call(functools.partial(tile_kernel, k), grid_spec=grid_spec, ou...  28.7 us
    all_to_all x1, blocking collectives, device_body(): lax.all_to_all(local, ('y', 'core'), split_axis=0, concat_axis=0, tiled=T...  16.7 us
    all_to_all x1, starting transfers between devices, device_body(): lax.all_to_all(mock_maps, 'col', split_axis=1, concat_axis=0, tiled=True)  4.35 us
  transfers between devices with their start and end apart: 3, of which 2 were waited for; matrix products, arithmetic and copies ran while one was open for 4% of the time, Pallas kernels for 8%

profile of v9, /device:TPU:1, one launch (start us, length us, event | category | flops | bytes accessed | tf_op | source)
XLA Modules:
  0.0 191.1 jit_solution(334325584008578779)
XLA Ops:
  6.5 0.0 copy-start
  6.5 0.0 all-gather.2.cloned.1.call-start
  6.5 1.4 fusion
  10.4 1.3 dynamic-slice_select_fusion.3
  11.8 0.0 copy-start.1
  11.8 1.3 reshape.30
  13.1 1.2 copy.28
  14.3 16.7 %all_to_all.25 = bf16[8,16,2560]{2,1,0:T(8,128)(2,1)S(1)} all-to-all(bf16[8,16,2560]{2,1,0:T(8,128)(2,1)S(1)} %bitcast.39), channel_id=1, replica_groups=mesh['y'=4,'core'=2,'col'=16] {'y','core'}, dimensions={0} | all-to-all | bytes 1310720 | tf_op jit(solution)/shard_map/all_to_all | solution.py:81
  30.9 0.7 reduce_sum.27
  31.6 0.0 all-gather.2.cloned.1.call-update
  31.7 69.5 %all-gather.2.cloned.1.call-done.b_ref = bf16[1024,2560]{1,0:T(8,128)(2,1)} async-done(((bf16[16,2560]{1,0:T(8,128)(2,1)}), bf16[1024,2560]{1,0:T(8,128)(2,1)}) %all-gather.2.cloned.1.call-update) | async-done | bytes 5242896 | tf_op jit(solution)/shard_map/all_gather | solution.py:83
  101.2 2.1 %collective-permute-start = (bf16[1024,2560]{1,0:T(8,128)(2,1)}, bf16[1024,2560]{1,0:T(8,128)(2,1)}, u32[]{:S(2)}, u32[]{:S(2)}) collective-permute-start(bf16[1024,2560]{1,0:T(8,128)(2,1)} %all-gather.2.cloned.1.call-done.b_ref), channel_id=1, source_target_pairs={{0,16},{16,0},{1,17},{17,1},{2,18},{18,2},{3,19},{19,3},{4,20},{20... | collective-permute-start | bytes 15728648 | tf_op jit(solution)/shard_map/ppermute | solution.py:84
  103.3 0.0 copy-done.1
  103.3 1.8 copy.37
  105.1 0.0 copy-start.2
  105.1 0.0 copy-start.3
  105.1 4.4 %all-to-all-start = ((bf16[64,16,1280]{2,0,1:T(8,128)(2,1)}), bf16[64,16,1280]{2,0,1:T(8,128)(2,1)S(1)}, u32[]{:S(2)}, u32[]{:S(2)}) async-start(bf16[64,16,1280]{2,0,1:T(8,128)(2,1)} %bitcast.35), calls=%async_computation | async-start | bytes 5242880 | tf_op jit(solution)/shard_map/all_to_all | solution.py:86
  109.4 0.0 copy-done.2
  109.4 0.0 copy-done.3
  109.5 0.2 select_reduce_fusion
  109.6 0.1 broadcast_bitcast_fusion.1
  109.7 0.0 copy-done
  109.8 0.1 broadcast_bitcast_fusion
  109.9 40.3 %all-to-all-done = bf16[64,16,1280]{2,0,1:T(8,128)(2,1)S(1)} async-done(((bf16[64,16,1280]{2,0,1:T(8,128)(2,1)}), bf16[64,16,1280]{2,0,1:T(8,128)(2,1)S(1)}, u32[]{:S(2)}, u32[]{:S(2)}) %all-to-all-start) | async-done | bytes 2621472 | tf_op jit(solution)/shard_map/all_to_all | solution.py:86
  150.2 0.5 convert_reduce_fusion
  150.6 0.2 broadcast_in_dim.28.rows_ref
  150.9 1.7 copy.27
  152.6 3.0 %copy.31.a_ref = bf16[1280,1024]{1,0:T(8,128)(2,1)S(1)} copy(bf16[1280,1024]{0,1:T(8,128)(2,1)} %bitcast.36) | data formatting | bytes 5242880 | tf_op jit(solution)/shard_map/reshape | solution.py:101
  155.6 14.4 %shard_map.55.rest_0_ = bf16[1280,5120]{1,0:T(8,128)(2,1)} custom-call(s32[1]{0:T(128)} %bitcast.13.off_ref, bf16[1280,1024]{1,0:T(8,128)(2,1)S(1)} %copy.31.a_ref, bf16[1024,2560]{1,0:T(8,128)(2,1)} %all-gather.2.cloned.1.call-done.b_ref, f32[1280,1]{1,0:T(8,128)S(1)} %broadcast_in_dim.28.rows_ref, f32[1,5120]{1,0:T(1,128)S(1)} %bitcast.30, ...), custom_call_target="tpu_custom_call" | custom-call | flops 6710886400 | bytes 14417920 | tf_op jit(solution)/shard_map/pallas_call | solution.py:49
  169.9 0.0 collective-permute-done.b_ref
  169.9 14.4 %shard_map.56 = bf16[1280,5120]{1,0:T(8,128)(2,1)} custom-call(s32[1]{0:T(128)} %bitcast.off_ref, bf16[1280,1024]{1,0:T(8,128)(2,1)S(1)} %copy.31.a_ref, bf16[1024,2560]{1,0:T(8,128)(2,1)} %collective-permute-done.b_ref, f32[1280,1]{1,0:T(8,128)S(1)} %broadcast_in_dim.28.rows_ref, f32[1,5120]{1,0:T(1,128)S(1)} %bitcast.31, ...), custom_call_target="tpu_custom_call", output_to_operand_aliasing={{}: (6, {})} | custom-call | flops 6710886400 | bytes 14417920 | tf_op jit(solution)/shard_map/pallas_call | solution.py:49
  (4 shorter events, 0.1 us)
Async XLA Ops:
  6.5 103.2 %copy-start = (s32[1,4]{1,0:T(1,128)S(1)}, s32[1,4]{1,0:T(1,128)}, u32[]{:S(2)}) copy-start(s32[1,4]{1,0:T(1,128)} %param.7) | copy-start | bytes 52
  6.5 94.6 %all-gather.2.cloned.1.call-start = ((), (), s32[]{:S(2)}) async-start(), calls=%async_computation.2 | async-start | bytes 5324800 | tf_op jit(solution)/shard_map/all_gather | solution.py:83
  11.8 91.5 %copy-start.1 = (bf16[64,20480]{1,0:T(8,128)(2,1)S(1)}, bf16[64,20480]{1,0:T(8,128)(2,1)}, u32[]{:S(2)}) copy-start(bf16[64,20480]{1,0:T(8,128)(2,1)} %param.5) | copy-start | bytes 7864324
  101.2 68.8 %collective-permute-start = (bf16[1024,2560]{1,0:T(8,128)(2,1)}, bf16[1024,2560]{1,0:T(8,128)(2,1)}, u32[]{:S(2)}, u32[]{:S(2)}) collective-permute-start(bf16[1024,2560]{1,0:T(8,128)(2,1)} %all-gather.2.cloned.1.call-done.b_ref), channel_id=1, source_target_pairs={{0,16},{16,0},{1,17},{17,1},{2,18},{18,2},{3,19},{19,3},{4,20},{20... | collective-permute-start | bytes 15728648 | tf_op jit(solution)/shard_map/ppermute | solution.py:84
  105.1 4.4 %copy-start.2 = (f32[4]{0:T(128)S(1)}, f32[4]{0:T(128)}, u32[]{:S(2)}) copy-start(f32[4]{0:T(128)} %param.9) | copy-start | bytes 52
  105.1 4.4 %copy-start.3 = (s32[1,4]{1,0:T(1,128)S(1)}, s32[1,4]{1,0:T(1,128)}, u32[]{:S(2)}) copy-start(s32[1,4]{1,0:T(1,128)} %param.8) | copy-start | bytes 52
  105.1 45.1 %all-to-all-start = ((bf16[64,16,1280]{2,0,1:T(8,128)(2,1)}), bf16[64,16,1280]{2,0,1:T(8,128)(2,1)S(1)}, u32[]{:S(2)}, u32[]{:S(2)}) async-start(bf16[64,16,1280]{2,0,1:T(8,128)(2,1)} %bitcast.35), calls=%async_computation | async-start | bytes 5242880 | tf_op jit(solution)/shard_map/all_to_all | solution.py:86
Sparse Core Ops, SparseCore 0:
  31.8 69.3 all-gather.1

commit v10 on v9

--- a/solution.py
+++ b/solution.py
@@ -74,12 +74,17 @@
         start = jnp.clip(local_id, 0, local_blocks - 1) * block_width
         piece = lax.dynamic_slice_in_dim(mock_maps, start, block_width, 1)
         chunks.append(jnp.where(mine, piece, jnp.zeros_like(piece)))
-    local = jnp.concatenate(chunks, axis=1)
-    m, n = local.shape
-    local = local.reshape(ny, m // ny, ncore, n // ncore).transpose(0, 2, 1, 3)
-    local = local.reshape(m * ncore, n // ncore)
+    per_half = WINDOW // ncore
+    halves = [
+        jnp.concatenate(chunks[hh * per_half:(hh + 1) * per_half], axis=1) for hh in range(ncore)
+    ]
+    m = mock_maps.shape[0]
+    rows_each = m // ny
+    local = jnp.stack(
+        [halves[hh][yy * rows_each:(yy + 1) * rows_each] for yy in range(ny) for hh in range(ncore)]
+    )
     sent = lax.all_to_all(local, ("y", "core"), split_axis=0, concat_axis=0, tiled=True)
-    part = jnp.sum(sent.reshape(ny * ncore, m // ny, n // ncore), axis=0, dtype=sent.dtype)
+    part = jnp.sum(sent, axis=0, dtype=sent.dtype)
     own_half = lax.all_gather(part, ("y", "col"), axis=0, tiled=True)
     other_half = lax.ppermute(own_half, "core", [(0, 1), (1, 0)])
 

time: 191 us -> 189 us (0.990)
  local copies, waits for them, and re-layouts: 10.8 us -> 8.29 us
where the time goes in v10:
time: 189 us
  waiting for transfers between devices  110 us (58%)
  Pallas kernels  28.7 us (15%)
  blocking collectives  16.8 us (9%)
  between operations  16 us (8%)
  local copies, waits for them, and re-layouts  8.29 us (4%)
  starting transfers between devices  6.5 us (3%)
  other arithmetic  2.72 us (1%)
    all_gather x1, waiting for transfers between devices, device_body(): own_half = lax.all_gather(part, ('y', 'col'), axis=0, tiled=True)  69.5 us
    all_to_all x1, waiting for transfers between devices, device_body(): lax.all_to_all(mock_maps, 'col', split_axis=1, concat_axis=0, tiled=True)  40.3 us
    pallas_call x2, Pallas kernels, half_tiles(): pl.pallas_call(functools.partial(tile_kernel, k), grid_spec=grid_spec, ou...  28.7 us
    all_to_all x1, blocking collectives, device_body(): lax.all_to_all(local, ('y', 'core'), split_axis=0, concat_axis=0, tiled=T...  16.8 us
    all_to_all x1, starting transfers between devices, device_body(): lax.all_to_all(mock_maps, 'col', split_axis=1, concat_axis=0, tiled=True)  4.35 us
  transfers between devices with their start and end apart: 3, of which 2 were waited for; matrix products, arithmetic and copies ran while one was open for 4% of the time, Pallas kernels for 8%

profile of v10, /device:TPU:1, one launch (start us, length us, event | category | flops | bytes accessed | tf_op | source)
XLA Modules:
  0.0 188.9 jit_solution(287503915406589775)
XLA Ops:
  6.5 0.0 copy-start
  6.5 0.0 all-gather.2.cloned.1.call-start
  6.5 1.4 fusion.22
  10.4 1.3 dynamic-slice_select_fusion
  11.7 0.0 copy-start.1
  11.9 16.8 %all_to_all.21 = bf16[8,16,2560]{2,1,0:T(8,128)(2,1)S(1)} all-to-all(bf16[8,16,2560]{2,1,0:T(8,128)(2,1)S(1)} %fusion.19), channel_id=1, replica_groups=mesh['y'=4,'core'=2,'col'=16] {'y','core'}, dimensions={0} | all-to-all | bytes 1310720 | tf_op jit(solution)/shard_map/all_to_all | solution.py:86
  28.7 0.7 reduce_sum.27
  29.4 0.0 all-gather.2.cloned.1.call-update
  29.4 69.5 %all-gather.2.cloned.1.call-done.b_ref = bf16[1024,2560]{1,0:T(8,128)(2,1)} async-done(((bf16[16,2560]{1,0:T(8,128)(2,1)}), bf16[1024,2560]{1,0:T(8,128)(2,1)}) %all-gather.2.cloned.1.call-update) | async-done | bytes 5242896 | tf_op jit(solution)/shard_map/all_gather | solution.py:88
  98.9 2.1 %collective-permute-start = (bf16[1024,2560]{1,0:T(8,128)(2,1)}, bf16[1024,2560]{1,0:T(8,128)(2,1)}, u32[]{:S(2)}, u32[]{:S(2)}) collective-permute-start(bf16[1024,2560]{1,0:T(8,128)(2,1)} %all-gather.2.cloned.1.call-done.b_ref), channel_id=1, source_target_pairs={{0,16},{16,0},{1,17},{17,1},{2,18},{18,2},{3,19},{19,3},{4,20},{20... | collective-permute-start | bytes 15728648 | tf_op jit(solution)/shard_map/ppermute | solution.py:89
  101.1 0.0 copy-done.1
  101.1 1.8 copy.34
  102.8 0.0 copy-start.2
  102.8 0.0 copy-start.3
  102.8 4.4 %all-to-all-start = ((bf16[64,16,1280]{2,0,1:T(8,128)(2,1)}), bf16[64,16,1280]{2,0,1:T(8,128)(2,1)S(1)}, u32[]{:S(2)}, u32[]{:S(2)}) async-start(bf16[64,16,1280]{2,0,1:T(8,128)(2,1)} %bitcast.65), calls=%async_computation | async-start | bytes 5242880 | tf_op jit(solution)/shard_map/all_to_all | solution.py:91
  107.2 0.0 copy-done.2
  107.2 0.0 copy-done.3
  107.2 0.2 select_reduce_fusion
  107.4 0.1 broadcast_bitcast_fusion.1
  107.5 0.0 copy-done
  107.5 0.1 broadcast_bitcast_fusion
  107.6 40.3 %all-to-all-done = bf16[64,16,1280]{2,0,1:T(8,128)(2,1)S(1)} async-done(((bf16[64,16,1280]{2,0,1:T(8,128)(2,1)}), bf16[64,16,1280]{2,0,1:T(8,128)(2,1)S(1)}, u32[]{:S(2)}, u32[]{:S(2)}) %all-to-all-start) | async-done | bytes 2621472 | tf_op jit(solution)/shard_map/all_to_all | solution.py:91
  147.9 0.5 convert_reduce_fusion
  148.4 0.2 broadcast_in_dim.28.rows_ref
  148.6 1.7 copy.25
  150.3 3.0 %copy.28.a_ref = bf16[1280,1024]{1,0:T(8,128)(2,1)S(1)} copy(bf16[1280,1024]{0,1:T(8,128)(2,1)} %bitcast.66) | data formatting | bytes 5242880 | tf_op jit(solution)/shard_map/reshape | solution.py:106
  153.3 14.4 %shard_map.55.rest_0_ = bf16[1280,5120]{1,0:T(8,128)(2,1)} custom-call(s32[1]{0:T(128)} %bitcast.19.off_ref, bf16[1280,1024]{1,0:T(8,128)(2,1)S(1)} %copy.28.a_ref, bf16[1024,2560]{1,0:T(8,128)(2,1)} %all-gather.2.cloned.1.call-done.b_ref, f32[1280,1]{1,0:T(8,128)S(1)} %broadcast_in_dim.28.rows_ref, f32[1,5120]{1,0:T(1,128)S(1)} %bitcast.60, ...), custom_call_target="tpu_custom_call" | custom-call | flops 6710886400 | bytes 14417920 | tf_op jit(solution)/shard_map/pallas_call | solution.py:49
  167.7 0.0 collective-permute-done.b_ref
  167.7 14.4 %shard_map.56 = bf16[1280,5120]{1,0:T(8,128)(2,1)} custom-call(s32[1]{0:T(128)} %bitcast.off_ref, bf16[1280,1024]{1,0:T(8,128)(2,1)S(1)} %copy.28.a_ref, bf16[1024,2560]{1,0:T(8,128)(2,1)} %collective-permute-done.b_ref, f32[1280,1]{1,0:T(8,128)S(1)} %broadcast_in_dim.28.rows_ref, f32[1,5120]{1,0:T(1,128)S(1)} %bitcast.61, ...), custom_call_target="tpu_custom_call", output_to_operand_aliasing={{}: (6, {})} | custom-call | flops 6710886400 | bytes 14417920 | tf_op jit(solution)/shard_map/pallas_call | solution.py:49
  (11 shorter events, 0.1 us)
Async XLA Ops:
  6.5 101.0 %copy-start = (s32[1,4]{1,0:T(1,128)S(1)}, s32[1,4]{1,0:T(1,128)}, u32[]{:S(2)}) copy-start(s32[1,4]{1,0:T(1,128)} %param.7) | copy-start | bytes 52
  6.5 92.4 %all-gather.2.cloned.1.call-start = ((), (), s32[]{:S(2)}) async-start(), calls=%async_computation.2 | async-start | bytes 5324800 | tf_op jit(solution)/shard_map/all_gather | solution.py:88
  11.7 89.3 %copy-start.1 = (bf16[64,20480]{1,0:T(8,128)(2,1)S(1)}, bf16[64,20480]{1,0:T(8,128)(2,1)}, u32[]{:S(2)}) copy-start(bf16[64,20480]{1,0:T(8,128)(2,1)} %param.5) | copy-start | bytes 7864324
  98.9 68.8 %collective-permute-start = (bf16[1024,2560]{1,0:T(8,128)(2,1)}, bf16[1024,2560]{1,0:T(8,128)(2,1)}, u32[]{:S(2)}, u32[]{:S(2)}) collective-permute-start(bf16[1024,2560]{1,0:T(8,128)(2,1)} %all-gather.2.cloned.1.call-done.b_ref), channel_id=1, source_target_pairs={{0,16},{16,0},{1,17},{17,1},{2,18},{18,2},{3,19},{19,3},{4,20},{20... | collective-permute-start | bytes 15728648 | tf_op jit(solution)/shard_map/ppermute | solution.py:89
  102.8 4.4 %copy-start.2 = (f32[4]{0:T(128)S(1)}, f32[4]{0:T(128)}, u32[]{:S(2)}) copy-start(f32[4]{0:T(128)} %param.9) | copy-start | bytes 52
  102.8 4.4 %copy-start.3 = (s32[1,4]{1,0:T(1,128)S(1)}, s32[1,4]{1,0:T(1,128)}, u32[]{:S(2)}) copy-start(s32[1,4]{1,0:T(1,128)} %param.8) | copy-start | bytes 52
  102.8 45.1 %all-to-all-start = ((bf16[64,16,1280]{2,0,1:T(8,128)(2,1)}), bf16[64,16,1280]{2,0,1:T(8,128)(2,1)S(1)}, u32[]{:S(2)}, u32[]{:S(2)}) async-start(bf16[64,16,1280]{2,0,1:T(8,128)(2,1)} %bitcast.65), calls=%async_computation | async-start | bytes 5242880 | tf_op jit(solution)/shard_map/all_to_all | solution.py:91
Sparse Core Ops, SparseCore 0:
  29.5 69.3 all-gather.1

commit v11 on v10

--- a/solution.py
+++ b/solution.py
@@ -67,13 +67,15 @@
     ncore = lax.axis_size("core")
     core = lax.axis_index("core")
     row = lax.axis_index("y") * ncore + core
-    chunks = []
-    for slot in range(WINDOW):
-        local_id = window_blocks[slot] - row * local_blocks
-        mine = (local_id >= 0) & (local_id < local_blocks)
-        start = jnp.clip(local_id, 0, local_blocks - 1) * block_width
-        piece = lax.dynamic_slice_in_dim(mock_maps, start, block_width, 1)
-        chunks.append(jnp.where(mine, piece, jnp.zeros_like(piece)))
+    blocks3 = mock_maps.reshape(mock_maps.shape[0], local_blocks, block_width)
+    local_ids = window_blocks - row * local_blocks
+    onehot = jnp.arange(local_blocks, dtype=jnp.int32)[None, :] == local_ids[:, None]
+    picked = jnp.sum(
+        jnp.where(onehot[None, :, :, None], blocks3[:, None, :, :], jnp.zeros((), blocks3.dtype)),
+        axis=2,
+        dtype=blocks3.dtype,
+    )
+    chunks = [picked[:, slot, :] for slot in range(WINDOW)]
     per_half = WINDOW // ncore
     halves = [
         jnp.concatenate(chunks[hh * per_half:(hh + 1) * per_half], axis=1) for hh in range(ncore)

time: 189 us -> 191 us (1.011)
  between operations: 16 us -> 13.6 us
  other arithmetic: 2.72 us -> 5.05 us
  local copies, waits for them, and re-layouts: 8.29 us -> 10.2 us
    reduce_sum x0 -> x1, other arithmetic: none -> 2.86 us  [device_body(): jnp.sum(jnp.where(onehot[None, :, :, None], blocks3[:, None, :, :], jnp.z...]
    unnamed x12 -> x15, local copies, waits for them, and re-layouts: 0.21 us -> 2.54 us
where the time goes in v11:
time: 191 us; the launch traced here: 190 us
  waiting for transfers between devices  110 us (58%)
  Pallas kernels  28.7 us (15%)
  blocking collectives  16.7 us (9%)
  between operations  13.6 us (7%)
  local copies, waits for them, and re-layouts  10.2 us (5%)
  starting transfers between devices  6.38 us (3%)
  other arithmetic  5.05 us (3%)
    all_gather x1, waiting for transfers between devices, device_body(): own_half = lax.all_gather(part, ('y', 'col'), axis=0, tiled=True)  69.5 us
    all_to_all x1, waiting for transfers between devices, device_body(): lax.all_to_all(mock_maps, 'col', split_axis=1, concat_axis=0, tiled=True)  40.3 us
    pallas_call x2, Pallas kernels, half_tiles(): pl.pallas_call(functools.partial(tile_kernel, k), grid_spec=grid_spec, ou...  28.7 us
    all_to_all x1, blocking collectives, device_body(): lax.all_to_all(local, ('y', 'core'), split_axis=0, concat_axis=0, tiled=T...  16.7 us
    all_to_all x1, starting transfers between devices, device_body(): lax.all_to_all(mock_maps, 'col', split_axis=1, concat_axis=0, tiled=True)  4.23 us
  transfers between devices with their start and end apart: 3, of which 2 were waited for; matrix products, arithmetic and copies ran while one was open for 4% of the time, Pallas kernels for 8%

profile of v11, /device:TPU:1, one launch (start us, length us, event | category | flops | bytes accessed | tf_op | source)
XLA Modules:
  0.0 190.3 jit_solution(11663111264430653467)
XLA Ops:
  6.5 0.0 copy-start
  6.5 0.0 all-gather.2.cloned.1.call-start
  6.5 0.7 broadcast_subtract_fusion
  7.2 0.1 iota_compare_fusion.1
  7.3 2.3 %copy.60 = bf16[8,8,16,1280]{3,2,1,0:T(8,128)(2,1)S(1)} copy(bf16[8,8,16,1280]{3,1,2,0:T(8,128)(2,1)} %bitcast.71) | data formatting | bytes 5242880
  9.5 2.9 %select_reduce_fusion = bf16[64,4,1280]{2,1,0:T(4,128)(2,1)S(1)} fusion(pred[4,16]{1,0:T(4,128)(4,1)S(1)} %iota_compare_fusion.1, bf16[64,16,1280]{2,1,0:T(8,128)(2,1)S(1)} %bitcast.74), kind=kLoop, calls=%fused_computation | loop fusion | flops 10158080 | bytes 3276864 | tf_op jit(solution)/shard_map/reduce_sum | solution.py:73
  12.4 0.0 copy-start.1
  12.4 0.9 fusion.22
  13.6 16.7 %all_to_all.21 = bf16[8,16,2560]{2,1,0:T(8,128)(2,1)S(1)} all-to-all(bf16[8,16,2560]{2,1,0:T(8,128)(2,1)S(1)} %fusion.19), channel_id=1, replica_groups=mesh['y'=4,'core'=2,'col'=16] {'y','core'}, dimensions={0} | all-to-all | bytes 1310720 | tf_op jit(solution)/shard_map/all_to_all | solution.py:88
  30.3 0.7 reduce_sum.37
  31.0 0.0 all-gather.2.cloned.1.call-update
  31.0 69.5 %all-gather.2.cloned.1.call-done.b_ref = bf16[1024,2560]{1,0:T(8,128)(2,1)} async-done(((bf16[16,2560]{1,0:T(8,128)(2,1)}), bf16[1024,2560]{1,0:T(8,128)(2,1)}) %all-gather.2.cloned.1.call-update) | async-done | bytes 5242896 | tf_op jit(solution)/shard_map/all_gather | solution.py:90
  100.5 2.1 %collective-permute-start = (bf16[1024,2560]{1,0:T(8,128)(2,1)}, bf16[1024,2560]{1,0:T(8,128)(2,1)}, u32[]{:S(2)}, u32[]{:S(2)}) collective-permute-start(bf16[1024,2560]{1,0:T(8,128)(2,1)} %all-gather.2.cloned.1.call-done.b_ref), channel_id=1, source_target_pairs={{0,16},{16,0},{1,17},{17,1},{2,18},{18,2},{3,19},{19,3},{4,20},{20... | collective-permute-start | bytes 15728648 | tf_op jit(solution)/shard_map/ppermute | solution.py:91
  102.7 0.0 copy-done.1
  102.7 0.0 copy-start.2
  102.7 0.0 copy-start.3
  102.7 1.8 copy.68
  104.4 4.2 %all-to-all-start = ((bf16[64,16,1280]{2,0,1:T(8,128)(2,1)}), bf16[64,16,1280]{2,0,1:T(8,128)(2,1)S(1)}, u32[]{:S(2)}, u32[]{:S(2)}) async-start(bf16[64,16,1280]{2,0,1:T(8,128)(2,1)} %bitcast.73), calls=%async_computation | async-start | bytes 5242880 | tf_op jit(solution)/shard_map/all_to_all | solution.py:93
  108.7 0.0 copy-done.2
  108.7 0.0 copy-done.3
  108.7 0.2 select_reduce_fusion.1
  108.9 0.1 broadcast_bitcast_fusion.1
  109.0 0.0 copy-done
  109.0 0.1 broadcast_bitcast_fusion
  109.1 40.3 %all-to-all-done = bf16[64,16,1280]{2,0,1:T(8,128)(2,1)S(1)} async-done(((bf16[64,16,1280]{2,0,1:T(8,128)(2,1)}), bf16[64,16,1280]{2,0,1:T(8,128)(2,1)S(1)}, u32[]{:S(2)}, u32[]{:S(2)}) %all-to-all-start) | async-done | bytes 2621472 | tf_op jit(solution)/shard_map/all_to_all | solution.py:93
  149.4 0.5 convert_reduce_fusion
  149.8 0.2 broadcast_in_dim.54.rows_ref
  150.1 1.7 copy.50
  151.8 3.0 %copy.53.a_ref = bf16[1280,1024]{1,0:T(8,128)(2,1)S(1)} copy(bf16[1280,1024]{0,1:T(8,128)(2,1)} %bitcast.75) | data formatting | bytes 5242880 | tf_op jit(solution)/shard_map/reshape | solution.py:108
  154.8 14.4 %shard_map.55.rest_0_ = bf16[1280,5120]{1,0:T(8,128)(2,1)} custom-call(s32[1]{0:T(128)} %bitcast.15.off_ref, bf16[1280,1024]{1,0:T(8,128)(2,1)S(1)} %copy.53.a_ref, bf16[1024,2560]{1,0:T(8,128)(2,1)} %all-gather.2.cloned.1.call-done.b_ref, f32[1280,1]{1,0:T(8,128)S(1)} %broadcast_in_dim.54.rows_ref, f32[1,5120]{1,0:T(1,128)S(1)} %bitcast.66, ...), custom_call_target="tpu_custom_call" | custom-call | flops 6710886400 | bytes 14417920 | tf_op jit(solution)/shard_map/pallas_call | solution.py:49
  169.1 0.0 collective-permute-done.b_ref
  169.1 14.4 %shard_map.56 = bf16[1280,5120]{1,0:T(8,128)(2,1)} custom-call(s32[1]{0:T(128)} %bitcast.off_ref, bf16[1280,1024]{1,0:T(8,128)(2,1)S(1)} %copy.53.a_ref, bf16[1024,2560]{1,0:T(8,128)(2,1)} %collective-permute-done.b_ref, f32[1280,1]{1,0:T(8,128)S(1)} %broadcast_in_dim.54.rows_ref, f32[1,5120]{1,0:T(1,128)S(1)} %bitcast.67, ...), custom_call_target="tpu_custom_call", output_to_operand_aliasing={{}: (6, {})} | custom-call | flops 6710886400 | bytes 14417920 | tf_op jit(solution)/shard_map/pallas_call | solution.py:49
  (13 shorter events, 0.2 us)
Async XLA Ops:
  6.5 102.4 %copy-start = (s32[1,4]{1,0:T(1,128)S(1)}, s32[1,4]{1,0:T(1,128)}, u32[]{:S(2)}) copy-start(s32[1,4]{1,0:T(1,128)} %param.7) | copy-start | bytes 52
  6.5 94.0 %all-gather.2.cloned.1.call-start = ((), (), s32[]{:S(2)}) async-start(), calls=%async_computation.2 | async-start | bytes 5324800 | tf_op jit(solution)/shard_map/all_gather | solution.py:90
  12.4 90.2 %copy-start.1 = (bf16[64,20480]{1,0:T(8,128)(2,1)S(1)}, bf16[64,20480]{1,0:T(8,128)(2,1)}, u32[]{:S(2)}) copy-start(bf16[64,20480]{1,0:T(8,128)(2,1)} %param.5) | copy-start | bytes 7864324
  100.5 68.6 %collective-permute-start = (bf16[1024,2560]{1,0:T(8,128)(2,1)}, bf16[1024,2560]{1,0:T(8,128)(2,1)}, u32[]{:S(2)}, u32[]{:S(2)}) collective-permute-start(bf16[1024,2560]{1,0:T(8,128)(2,1)} %all-gather.2.cloned.1.call-done.b_ref), channel_id=1, source_target_pairs={{0,16},{16,0},{1,17},{17,1},{2,18},{18,2},{3,19},{19,3},{4,20},{20... | collective-permute-start | bytes 15728648 | tf_op jit(solution)/shard_map/ppermute | solution.py:91
  102.7 6.0 %copy-start.2 = (f32[4]{0:T(128)S(1)}, f32[4]{0:T(128)}, u32[]{:S(2)}) copy-start(f32[4]{0:T(128)} %param.9) | copy-start | bytes 52
  102.7 6.0 %copy-start.3 = (s32[1,4]{1,0:T(1,128)S(1)}, s32[1,4]{1,0:T(1,128)}, u32[]{:S(2)}) copy-start(s32[1,4]{1,0:T(1,128)} %param.8) | copy-start | bytes 52
  104.4 44.9 %all-to-all-start = ((bf16[64,16,1280]{2,0,1:T(8,128)(2,1)}), bf16[64,16,1280]{2,0,1:T(8,128)(2,1)S(1)}, u32[]{:S(2)}, u32[]{:S(2)}) async-start(bf16[64,16,1280]{2,0,1:T(8,128)(2,1)} %bitcast.73), calls=%async_computation | async-start | bytes 5242880 | tf_op jit(solution)/shard_map/all_to_all | solution.py:93
Sparse Core Ops, SparseCore 0:
  31.1 69.3 all-gather.1

commit v12 on v10

--- a/solution.py
+++ b/solution.py
@@ -9,18 +9,23 @@
 from jax.sharding import PartitionSpec as P
 
 WINDOW = 4
-TILE_N = 1280
+TILE_N = 2560
+ROW_CHUNK = 128
 
 
 def tile_kernel(mock_count, off_ref, a_ref, b_ref, rows_ref, w_ref, keep_ref, *rest):
     o_ref = rest[-1]
     b = b_ref[...]
-    prod = jnp.dot(a_ref[...], b, preferred_element_type=jnp.float32)
     ones = jnp.ones((8, b.shape[0]), b.dtype)
-    col_sum = jnp.dot(ones, b, preferred_element_type=jnp.float32)[0:1, :]
-    centred = prod - rows_ref[...] * (col_sum / mock_count)
-    val = centred * w_ref[...]
-    o_ref[...] = jnp.where(keep_ref[...] > 0, val, jnp.float32(0.0)).astype(o_ref.dtype)
+    col_mean = jnp.dot(ones, b, preferred_element_type=jnp.float32)[0:1, :] / mock_count
+    scale = w_ref[...]
+    keep = keep_ref[...] > 0
+    for r in range(0, a_ref.shape[0], ROW_CHUNK):
+        rows = pl.ds(r, ROW_CHUNK)
+        prod = jnp.dot(a_ref[rows, :], b, preferred_element_type=jnp.float32)
+        centred = prod - rows_ref[rows, :] * col_mean
+        val = centred * scale
+        o_ref[rows, :] = jnp.where(keep, val, jnp.float32(0.0)).astype(o_ref.dtype)
 
 
 def half_tiles(offset, own_t, panels_half, row_sums, weight_cols, keep_cols, prev=None):

time: 189 us -> 187 us (0.989)
  Pallas kernels: 28.7 us -> 26.4 us
    pallas_call x2, Pallas kernels: 28.7 us -> 26.4 us  [half_tiles(): pl.pallas_call(functools.partial(tile_kernel, k), grid_spec=grid_spec, ou...]
  transfers between devices with their start and end apart: 3 -> 3, of which waited for: 2 -> 2; matrix products, arithmetic and copies ran while one was open for 4% -> 4% of each run, Pallas kernels for 8% -> 7%
where the time goes in v12:
time: 187 us
  waiting for transfers between devices  110 us (59%)
  Pallas kernels  26.4 us (14%)
  blocking collectives  16.8 us (9%)
  between operations  16 us (9%)
  local copies, waits for them, and re-layouts  8.48 us (5%)
  starting transfers between devices  6.5 us (3%)
  other arithmetic  2.72 us (1%)
    all_gather x1, waiting for transfers between devices, device_body(): own_half = lax.all_gather(part, ('y', 'col'), axis=0, tiled=True)  69.5 us
    all_to_all x1, waiting for transfers between devices, device_body(): lax.all_to_all(mock_maps, 'col', split_axis=1, concat_axis=0, tiled=True)  40.3 us
    pallas_call x2, Pallas kernels, half_tiles(): pl.pallas_call(functools.partial(tile_kernel, k), grid_spec=grid_spec, ou...  26.4 us
    all_to_all x1, blocking collectives, device_body(): lax.all_to_all(local, ('y', 'core'), split_axis=0, concat_axis=0, tiled=T...  16.8 us
    all_to_all x1, starting transfers between devices, device_body(): lax.all_to_all(mock_maps, 'col', split_axis=1, concat_axis=0, tiled=True)  4.35 us
  transfers between devices with their start and end apart: 3, of which 2 were waited for; matrix products, arithmetic and copies ran while one was open for 4% of the time, Pallas kernels for 7%

profile of v12, /device:TPU:1, one launch (start us, length us, event | category | flops | bytes accessed | tf_op | source)
XLA Modules:
  0.0 186.7 jit_solution(11783265160381473643)
XLA Ops:
  6.5 0.0 copy-start
  6.5 0.0 all-gather.2.cloned.1.call-start
  6.5 1.4 fusion.22
  10.4 1.3 dynamic-slice_select_fusion
  11.7 0.0 copy-start.1
  11.9 16.8 %all_to_all.21 = bf16[8,16,2560]{2,1,0:T(8,128)(2,1)S(1)} all-to-all(bf16[8,16,2560]{2,1,0:T(8,128)(2,1)S(1)} %fusion.19), channel_id=1, replica_groups=mesh['y'=4,'core'=2,'col'=16] {'y','core'}, dimensions={0} | all-to-all | bytes 1310720 | tf_op jit(solution)/shard_map/all_to_all | solution.py:91
  28.7 0.7 reduce_sum.27
  29.4 0.0 all-gather.2.cloned.1.call-update
  29.4 69.5 %all-gather.2.cloned.1.call-done.b_ref = bf16[1024,2560]{1,0:T(8,128)(2,1)} async-done(((bf16[16,2560]{1,0:T(8,128)(2,1)}), bf16[1024,2560]{1,0:T(8,128)(2,1)}) %all-gather.2.cloned.1.call-update) | async-done | bytes 5242896 | tf_op jit(solution)/shard_map/all_gather | solution.py:93
  98.9 2.1 %collective-permute-start = (bf16[1024,2560]{1,0:T(8,128)(2,1)}, bf16[1024,2560]{1,0:T(8,128)(2,1)}, u32[]{:S(2)}, u32[]{:S(2)}) collective-permute-start(bf16[1024,2560]{1,0:T(8,128)(2,1)} %all-gather.2.cloned.1.call-done.b_ref), channel_id=1, source_target_pairs={{0,16},{16,0},{1,17},{17,1},{2,18},{18,2},{3,19},{19,3},{4,20},{20... | collective-permute-start | bytes 15728648 | tf_op jit(solution)/shard_map/ppermute | solution.py:94
  101.1 0.0 copy-done.1
  101.1 1.8 copy.34
  102.8 0.0 copy-start.2
  102.8 0.0 copy-start.3
  102.8 4.4 %all-to-all-start = ((bf16[64,16,1280]{2,0,1:T(8,128)(2,1)}), bf16[64,16,1280]{2,0,1:T(8,128)(2,1)S(1)}, u32[]{:S(2)}, u32[]{:S(2)}) async-start(bf16[64,16,1280]{2,0,1:T(8,128)(2,1)} %bitcast.65), calls=%async_computation | async-start | bytes 5242880 | tf_op jit(solution)/shard_map/all_to_all | solution.py:96
  107.2 0.0 copy-done.2
  107.2 0.0 copy-done.3
  107.2 0.2 select_reduce_fusion
  107.4 0.1 broadcast_bitcast_fusion.1
  107.5 0.0 copy-done
  107.5 0.1 broadcast_bitcast_fusion
  107.6 40.3 %all-to-all-done = bf16[64,16,1280]{2,0,1:T(8,128)(2,1)S(1)} async-done(((bf16[64,16,1280]{2,0,1:T(8,128)(2,1)}), bf16[64,16,1280]{2,0,1:T(8,128)(2,1)S(1)}, u32[]{:S(2)}, u32[]{:S(2)}) %all-to-all-start) | async-done | bytes 2621472 | tf_op jit(solution)/shard_map/all_to_all | solution.py:96
  147.9 0.5 convert_reduce_fusion
  148.4 0.2 broadcast_in_dim.28.rows_ref
  148.6 1.7 copy.25
  150.3 3.2 %copy.28.a_ref = bf16[1280,1024]{1,0:T(8,128)(2,1)S(1)} copy(bf16[1280,1024]{0,1:T(8,128)(2,1)} %bitcast.66) | data formatting | bytes 5242880 | tf_op jit(solution)/shard_map/reshape | solution.py:111
  153.5 13.1 %shard_map.55.rest_0_ = bf16[1280,5120]{1,0:T(8,128)(2,1)} custom-call(s32[1]{0:T(128)} %bitcast.19.off_ref, bf16[1280,1024]{1,0:T(8,128)(2,1)S(1)} %copy.28.a_ref, bf16[1024,2560]{1,0:T(8,128)(2,1)} %all-gather.2.cloned.1.call-done.b_ref, f32[1280,1]{1,0:T(8,128)S(1)} %broadcast_in_dim.28.rows_ref, f32[1,5120]{1,0:T(1,128)S(1)} %bitcast.60, ...), custom_call_target="tpu_custom_call" | custom-call | flops 6710886400 | bytes 14417920 | tf_op jit(solution)/shard_map/pallas_call | solution.py:54
  166.5 0.0 collective-permute-done.b_ref
  166.6 13.3 %shard_map.56 = bf16[1280,5120]{1,0:T(8,128)(2,1)} custom-call(s32[1]{0:T(128)} %bitcast.off_ref, bf16[1280,1024]{1,0:T(8,128)(2,1)S(1)} %copy.28.a_ref, bf16[1024,2560]{1,0:T(8,128)(2,1)} %collective-permute-done.b_ref, f32[1280,1]{1,0:T(8,128)S(1)} %broadcast_in_dim.28.rows_ref, f32[1,5120]{1,0:T(1,128)S(1)} %bitcast.61, ...), custom_call_target="tpu_custom_call", output_to_operand_aliasing={{}: (6, {})} | custom-call | flops 6710886400 | bytes 14417920 | tf_op jit(solution)/shard_map/pallas_call | solution.py:54
  (11 shorter events, 0.1 us)
Async XLA Ops:
  6.5 101.0 %copy-start = (s32[1,4]{1,0:T(1,128)S(1)}, s32[1,4]{1,0:T(1,128)}, u32[]{:S(2)}) copy-start(s32[1,4]{1,0:T(1,128)} %param.7) | copy-start | bytes 52
  6.5 92.4 %all-gather.2.cloned.1.call-start = ((), (), s32[]{:S(2)}) async-start(), calls=%async_computation.2 | async-start | bytes 5324800 | tf_op jit(solution)/shard_map/all_gather | solution.py:93
  11.7 89.3 %copy-start.1 = (bf16[64,20480]{1,0:T(8,128)(2,1)S(1)}, bf16[64,20480]{1,0:T(8,128)(2,1)}, u32[]{:S(2)}) copy-start(bf16[64,20480]{1,0:T(8,128)(2,1)} %param.5) | copy-start | bytes 7864324
  98.9 67.6 %collective-permute-start = (bf16[1024,2560]{1,0:T(8,128)(2,1)}, bf16[1024,2560]{1,0:T(8,128)(2,1)}, u32[]{:S(2)}, u32[]{:S(2)}) collective-permute-start(bf16[1024,2560]{1,0:T(8,128)(2,1)} %all-gather.2.cloned.1.call-done.b_ref), channel_id=1, source_target_pairs={{0,16},{16,0},{1,17},{17,1},{2,18},{18,2},{3,19},{19,3},{4,20},{20... | collective-permute-start | bytes 15728648 | tf_op jit(solution)/shard_map/ppermute | solution.py:94
  102.8 4.4 %copy-start.2 = (f32[4]{0:T(128)S(1)}, f32[4]{0:T(128)}, u32[]{:S(2)}) copy-start(f32[4]{0:T(128)} %param.9) | copy-start | bytes 52
  102.8 4.4 %copy-start.3 = (s32[1,4]{1,0:T(1,128)S(1)}, s32[1,4]{1,0:T(1,128)}, u32[]{:S(2)}) copy-start(s32[1,4]{1,0:T(1,128)} %param.8) | copy-start | bytes 52
  102.8 45.1 %all-to-all-start = ((bf16[64,16,1280]{2,0,1:T(8,128)(2,1)}), bf16[64,16,1280]{2,0,1:T(8,128)(2,1)S(1)}, u32[]{:S(2)}, u32[]{:S(2)}) async-start(bf16[64,16,1280]{2,0,1:T(8,128)(2,1)} %bitcast.65), calls=%async_computation | async-start | bytes 5242880 | tf_op jit(solution)/shard_map/all_to_all | solution.py:96
Sparse Core Ops, SparseCore 0:
  29.5 69.3 all-gather.1
